TPU v7x, 32 devices: a whole 2x2x4 slice. The times are simulated.
32 devices in a mesh: groups: 2 (over y), range: 8 (over z, x), chan: 2 (over core).
Axes of the slice: x: 2, y: 2, z: 4, core: 2. Of those that a mesh axis runs over, the one named last changes fastest.
Arguments:
- echoes: bfloat16 [4, 512, 8, 1024], P('groups', 'chan', None, 'range'), parts along dimension 0, may hold values from -6 to 6
- chirp: float32 [2, 2049], replicated, may hold values from -0.09375 to 0.09375
- gates: int32 [4, 8], P('groups'), parts along dimension 0, may hold values from 0 to 1023, as said below
Outputs:
- compressed: bfloat16 [4, 512, 8, 1024], P('groups', 'chan', None, 'range'), parts along dimension 0
- covariance: float32 [4, 2, 2048, 4096], P('groups', 'chan', 'range'), parts along dimension 0
There are 2 independent parts, one for each index of `groups`. A program takes and returns all parts, laid end to end along the dimension named above; an argument that names none is the same for every part. Nothing has to cross between parts.
Inputs may be any that keep to these rules, and one draw needn't show every extreme that they name: `gates`: the 8 intervals are given in increasing order, do not intersect, lie within the 1024 cells, each holds one cell or more, and their lengths add up to 128. The first interval starts at cell 0, and the last is the single cell 1024 - 1.
All inputs are finite; a program needn't handle non-finite values.
Results may differ from a plain program's by a relative error of at most 0.0035.
Values may be sent and summed in bfloat16 or wider, within the bound.
No kernel may reach another device: no remote copies, remote signals or barrier semaphores. Data moves between devices by JAX's collectives and lax.ppermute only.
A program may use at most 128 MiB of HBM per device.

v0:
```python
from functools import partial
import math

import jax
import jax.numpy as jnp
from jax import lax
from jax.sharding import PartitionSpec as P

TRAIN = 128


def partner_2(value, axis, bit):
    mask = 2**bit
    pairs = [(source, source ^ mask) for source in range(lax.axis_size(axis))]
    return lax.ppermute(value, axis, pairs)


def as_sent(x):

    def short(part):
        return part.astype(jnp.bfloat16) if part.dtype == jnp.float32 else part

    return jax.tree.map(short, x)


def train_cells(gates, count):
    starts = gates[0]
    widths = gates[1]
    ends = jnp.cumsum(widths)
    places = jnp.arange(count, dtype=jnp.int32)
    which = jnp.sum((ends[None, :] <= places[:, None]).astype(jnp.int32), axis=1)
    onehot = jnp.arange(gates.shape[1], dtype=jnp.int32)[None, :] == which[:, None]
    offset = jnp.sum(jnp.where(onehot, (starts - (ends - widths))[None, :], 0), axis=1)
    return offset + places


def angle_tables(radix, nfft, sign):
    steps = jnp.arange(radix, dtype=jnp.int32)
    square = steps[:, None] * steps[None, :]
    small = sign * 2.0 * math.pi * (square % radix).astype(jnp.float32) / radix
    large = sign * 2.0 * math.pi * square.astype(jnp.float32) / nfft
    small_cos = jnp.cos(small)
    small_sin = jnp.sin(small)
    stacked = jnp.stack([small_cos, small_sin])
    block = jnp.concatenate(
        [
            jnp.concatenate([small_cos, small_sin], axis=1),
            jnp.concatenate([-small_sin, small_cos], axis=1),
        ],
        axis=0,
    )
    twiddle = jnp.concatenate([jnp.cos(large), jnp.sin(large)], axis=1)
    return (stacked, block, twiddle)


def merged_times(first, second):
    half = first.shape[-1] // 2
    first_re = first[..., :half]
    first_im = first[..., half:]
    second_re = second[..., :half]
    second_im = second[..., half:]
    return jnp.concatenate(
        [first_re * second_re - first_im * second_im, first_re * second_im + first_im * second_re],
        axis=-1,
    )


def left_section(stacked, values):
    mixed = jnp.einsum("ckn,...nr->...ckr", stacked, values, precision=lax.Precision.HIGHEST)
    half = values.shape[-1] // 2
    real_part = mixed[..., 0, :, :half] - mixed[..., 1, :, half:]
    imag_part = mixed[..., 1, :, :half] + mixed[..., 0, :, half:]
    return jnp.concatenate([real_part, imag_part], axis=-1)


def right_section(values, block):
    return jnp.einsum("...km,mj->...kj", values, block, precision=lax.Precision.HIGHEST)


def forward_dft(values, tables):
    stacked, block, twiddle = tables
    section = left_section(stacked, values)
    section = merged_times(section, twiddle)
    return right_section(section, block)


def inverse_upper(spectrum, tables):
    stacked, block, twiddle = tables
    section = right_section(spectrum, block)
    section = merged_times(section, twiddle)
    half = stacked.shape[1] // 2
    return left_section(stacked[:, half:], section)


def gram(left, right):
    contract = partial(
        lax.dot_general,
        dimension_numbers=(((1,), (1,)), ((), ())),
        preferred_element_type=jnp.float32,
    )
    real_part = contract(left[0], right[0]) + contract(left[1], right[1])
    imag_part = contract(left[1], right[0]) - contract(left[0], right[1])
    return jnp.stack([real_part, imag_part])


def on_device(echoes, chirp, gates):
    chans = echoes.shape[1]
    pulses = echoes.shape[2]
    cells_dev = echoes.shape[3]
    taps = chirp.shape[1]
    newlen = taps - 1
    nfft = 2 * newlen
    radix = math.isqrt(nfft)
    ranks = lax.axis_size("range")
    range_len = cells_dev * ranks
    nseg = (range_len + newlen - 1) // newlen
    forward_tables = angle_tables(radix, nfft, -1.0)
    inverse_tables = angle_tables(radix, nfft, 1.0)
    padded_taps = jnp.pad(chirp, ((0, 0), (0, nfft - taps))).reshape(2, radix, radix)
    response = forward_dft(
        jnp.concatenate([padded_taps[0], padded_taps[1]], axis=-1), forward_tables
    )
    series_total = chans * pulses
    local = echoes.reshape(2, series_total, cells_dev)
    cells = train_cells(gates, TRAIN)
    series_all = lax.all_to_all(local, "range", split_axis=1, concat_axis=2, tiled=True)
    values = series_all.astype(jnp.float32)
    count = values.shape[1]
    padded = jnp.pad(values, ((0, 0), (0, 0), (newlen, nseg * newlen - range_len)))
    blocks = padded.reshape(2, count, nseg + 1, newlen)
    frames = jnp.concatenate([blocks[:, :, :-1], blocks[:, :, 1:]], axis=3).reshape(
        2, count, nseg, radix, radix
    )
    merged = jnp.concatenate([frames[0], frames[1]], axis=-1)
    spectrum = forward_dft(merged, forward_tables)
    shaped = merged_times(spectrum, response)
    outcome = inverse_upper(shaped, inverse_tables)
    out_re = outcome[..., :radix].reshape(count, -1)[:, :range_len] / nfft
    out_im = outcome[..., radix:].reshape(count, -1)[:, :range_len] / nfft
    filtered = jnp.stack([out_re, out_im]).astype(jnp.bfloat16)
    returned = lax.all_to_all(filtered, "range", split_axis=2, concat_axis=1, tiled=True)
    compressed = returned.reshape(2, chans, pulses, cells_dev)
    snapshots = jnp.take(filtered, cells, axis=2)
    partner = partner_2(snapshots, "chan", 0)
    upper = lax.axis_index("chan") == 0
    series_dev = snapshots.shape[1]
    piece = lax.all_gather(snapshots, "range", axis=1, tiled=True)
    joined = jnp.stack([gram(snapshots, piece), gram(partner, piece)], axis=1)
    own_rows = joined[:, 0]
    cross_rows = joined[:, 1]
    other_rows = partner_2(as_sent(cross_rows), "chan", 0).astype(cross_rows.dtype)
    rows_out = jnp.where(
        upper,
        jnp.concatenate([own_rows, other_rows], axis=2),
        jnp.concatenate([other_rows, own_rows], axis=2),
    )
    covariance = (rows_out / TRAIN).reshape(2, 1, series_dev, -1)
    return (compressed, covariance)


def solution(mesh):
    placed = (P("groups", "chan", None, "range"), P(), P("groups", None))
    return jax.shard_map(
        on_device,
        mesh=mesh,
        in_specs=placed,
        out_specs=(P("groups", "chan", None, "range"), P("groups", "chan", "range", None)),
        check_vma=False,
    )
```

profile of v0, /device:TPU:0, one launch (start us, length us, event | category | flops | bytes accessed | tf_op | source)
XLA Modules:
  0.0 279.2 jit_solution(12653052795058454825)
XLA Ops:
  7.2 3.8 %copy.130 = bf16[2,256,8,128]{3,0,2,1:T(2,128)(2,1)} copy(bf16[2,256,8,128]{3,2,1,0:T(8,128)(2,1)} %param.3) | data formatting | bytes 2097152 | tf_op args[0]
  11.0 7.3 %all-to-all-start = ((bf16[2,2048,128]{2,0,1:T(2,128)(2,1)}), bf16[2,2048,128]{2,0,1:T(2,128)(2,1)S(1)}, u32[]{:S(2)}, u32[]{:S(2)}) async-start(bf16[2,2048,128]{2,0,1:T(2,128)(2,1)} %bitcast), calls=%async_computation | async-start | bytes 2097152 | tf_op jit(solution)/shard_map/all_to_all | solution.py:126
  20.4 0.4 fusion.60
  20.9 0.3 fusion.40
  21.6 22.4 %all-to-all-done = bf16[2,2048,128]{2,0,1:T(2,128)(2,1)S(1)} async-done(((bf16[2,2048,128]{2,0,1:T(2,128)(2,1)}), bf16[2,2048,128]{2,0,1:T(2,128)(2,1)S(1)}, u32[]{:S(2)}, u32[]{:S(2)}) %all-to-all-start) | async-done | bytes 1048608 | tf_op jit(solution)/shard_map/all_to_all | solution.py:126
  44.2 1.1 copy.132
  45.2 0.3 pad.9
  45.5 0.7 fusion.95
  46.3 3.7 %fusion.12 = (f32[1,256,1,4096]{1,3,2,0:T(8,128)}, f32[1,256,1,4096]{1,3,2,0:T(8,128)}) fusion(f32[2,256,1,2048]{1,3,2,0:T(8,128)S(1)} %get-tuple-element.26, f32[2,256,1,2048]{1,3,2,0:T(8,128)S(1)} %get-tuple-element.27), kind=kLoop, calls=%fused_computation.26 | loop fusion | flops 2097152 | bytes 16777216 | tf_op jit(solution)/shard_map/concatenate | solution.py:131
  49.9 9.1 %copy.133 = f32[256,1,64,64]{3,2,0,1:T(8,128)} copy(f32[256,1,64,64]{0,3,2,1:T(8,128)} %bitcast.180) | data formatting | bytes 8388608 | tf_op jit(solution)/shard_map/squeeze | solution.py:134
  59.1 9.1 %copy.134 = f32[256,1,64,64]{3,2,0,1:T(8,128)} copy(f32[256,1,64,64]{0,3,2,1:T(8,128)} %bitcast.179) | data formatting | bytes 8388608 | tf_op jit(solution)/shard_map/squeeze | solution.py:134
  68.2 20.8 %convolution_bitcast_fusion = f32[256,1,2,64,128]{4,3,2,0,1:T(8,128)} fusion(f32[256,1,64,64]{3,2,0,1:T(8,128)} %copy.134, f32[256,1,64,64]{3,2,0,1:T(8,128)} %copy.133, f32[1,64,64]{2,1,0:T(8,128)S(1)} %get-tuple-element.38, f32[1,64,64]{2,1,0:T(8,128)S(1)} %get-tuple-element.39), kind=kOutput, calls=%fused_computation.1 | convolution fusion | flops 3223330816 | bytes 25198592 | tf_op jit(solution)/shard_map/ckn,...nr->...ckr/dot_general | solution.py:69
  89.0 19.7 %multiply_subtract_fusion = (f32[256,1,64,64]{3,2,0,1:T(8,128)}, f32[256,1,64,64]{3,2,0,1:T(8,128)}) fusion(f32[64,64]{1,0:T(8,128)S(1)} %copy.138, f32[64,64]{1,0:T(8,128)S(1)} %copy.137, f32[256,1,2,64,128]{4,3,2,0,1:T(8,128)} %convolution_bitcast_fusion), kind=kLoop, calls=%fused_computation.25 | loop fusion | flops 8388608 | bytes 25198592 | tf_op jit(solution)/shard_map/sub | solution.py:63
  108.7 11.9 %maximum_bitcast_fusion.2 = f32[256,64,128]{2,1,0:T(8,128)} fusion(f32[256,1,64,64]{3,2,0,1:T(8,128)} %get-tuple-element.17, f32[256,1,64,64]{3,2,0,1:T(8,128)} %get-tuple-element.16), kind=kLoop, calls=%fused_computation.13 | loop fusion | flops 2097152 | bytes 16777216 | tf_op jit(solution)/shard_map/reshape.22
  120.6 16.0 %fusion.13 = f32[256,1,64,128]{0,3,2,1:T(8,128)S(1)} fusion(f32[256,64,128]{2,1,0:T(8,128)} %maximum_bitcast_fusion.2, f32[64,64]{0,1:T(8,128)S(1)} %get-tuple-element.41, f32[64,64]{0,1:T(8,128)S(1)} %fusion.84, f32[64,64]{0,1:T(8,128)S(1)} %get-tuple-element.40), kind=kOutput, calls=%fused_computation.35 | convolution fusion | flops 3221274624 | bytes 16826368 | tf_op jit(solution)/shard_map/...km,mj->...kj/dot_general | solution.py:77
  136.6 1.7 multiply_subtract_fusion.2
  138.2 8.5 %fusion.16 = f32[256,1,64,128]{0,3,2,1:T(8,128)S(1)} fusion(f32[256,1,64,64]{0,3,2,1:T(8,128)S(1)} %get-tuple-element.21, f32[256,1,64,64]{0,3,2,1:T(8,128)S(1)} %get-tuple-element.20, f32[64,64]{0,1:T(8,128)S(1)} %get-tuple-element.43, f32[64,64]{0,1:T(8,128)S(1)} %fusion.85, f32[64,64]{0,1:T(8,128)S(1)} %get-tuple-element.42), kind=kOutput, calls=%fused_computation.37 | convolution fusion | flops 3223371776 | bytes 16826368 | tf_op jit(solution)/shard_map/...km,mj->...kj/dot_general | solution.py:77
  146.8 1.5 multiply_subtract_fusion.1
  148.3 4.0 %maximum_bitcast_fusion.5 = f32[256,64,128,1]{0,2,1,3:T(8,128)} fusion(f32[256,1,64,64]{0,3,2,1:T(8,128)S(1)} %get-tuple-element.19, f32[256,1,64,64]{0,3,2,1:T(8,128)S(1)} %get-tuple-element.18), kind=kLoop, calls=%fused_computation.18 | loop fusion | flops 2097152 | bytes 16777216 | tf_op jit(solution)/shard_map/reshape.38
  152.3 8.7 %copy.165 = f32[256,64,128,1]{2,1,3,0:T(8,128)} copy(f32[256,64,128,1]{0,2,1,3:T(8,128)} %maximum_bitcast_fusion.5) | data formatting | bytes 16777216 | tf_op jit(solution)/shard_map/reshape.38
  161.0 12.6 %convolution_bitcast_fusion.1 = f32[256,1,2,32,128]{4,3,2,0,1:T(8,128)} fusion(f32[256,64,128,1]{2,1,3,0:T(8,128)} %copy.165, f32[1,64,64]{2,1,0:T(8,128)S(1)} %get-tuple-element.44, f32[1,64,64]{2,1,0:T(8,128)S(1)} %get-tuple-element.45), kind=kOutput, calls=%fused_computation.36 | convolution fusion | flops 1610616832 | bytes 16809984 | tf_op jit(solution)/shard_map/ckn,...nr->...ckr/dot_general | solution.py:69
  173.6 11.4 %slice_subtract_fusion = (f32[256,1,1,32,64]{4,3,2,0,1:T(8,128)}, f32[256,1,1,32,64]{4,3,2,0,1:T(8,128)}) fusion(f32[256,1,2,32,128]{4,3,2,0,1:T(8,128)} %convolution_bitcast_fusion.1), kind=kLoop, calls=%fused_computation.28 | loop fusion | flops 1048576 | bytes 12582912 | tf_op jit(solution)/shard_map/sub | solution.py:71
  184.9 3.5 %copy.148 = f32[256,1,1,32,64]{0,4,3,2,1:T(8,128)S(1)} copy(f32[256,1,1,32,64]{4,3,2,0,1:T(8,128)} %get-tuple-element.22) | data formatting | bytes 4194304 | tf_op jit(solution)/shard_map/sub | solution.py:71
  188.6 0.8 copy.152
  189.4 3.6 %copy.150 = f32[256,1,1,32,64]{0,4,3,2,1:T(8,128)S(1)} copy(f32[256,1,1,32,64]{4,3,2,0,1:T(8,128)} %get-tuple-element.23) | data formatting | bytes 4194304 | tf_op jit(solution)/shard_map/add | solution.py:72
  193.0 0.8 copy.153
  193.9 3.4 %pad_maximum_fusion.2 = bf16[2,256,1024]{1,0,2:T(2,128)(2,1)} fusion(bf16[1,256,1024]{1,0,2:T(2,128)(2,1)S(1)} %copy.153, bf16[1,256,1024]{1,0,2:T(2,128)(2,1)S(1)} %copy.152), kind=kLoop, calls=%fused_computation.54 | loop fusion | flops 2097152 | bytes 2097152 | tf_op jit(solution)/shard_map/stack | solution.py:140
  197.2 2.1 gather_fusion
  199.3 0.9 fusion.39
  200.3 4.3 %all-to-all-start.1 = ((bf16[2,256,1024]{1,0,2:T(2,128)(2,1)}), bf16[2,256,1024]{1,0,2:T(2,128)(2,1)}, u32[]{:S(2)}, u32[]{:S(2)}) async-start(bf16[2,256,1024]{1,0,2:T(2,128)(2,1)} %pad_maximum_fusion.2), calls=%async_computation.1 | async-start | bytes 2097152 | tf_op jit(solution)/shard_map/all_to_all | solution.py:141
  204.6 0.2 fusion.98
  205.1 45.5 %all-gather.2.cloned.1.call-done = bf16[2,2048,128]{1,0,2:T(2,128)(2,1)} async-done(((bf16[2,256,128]{1,0,2:T(2,128)(2,1)}), bf16[2,2048,128]{1,0,2:T(2,128)(2,1)}) %all-gather.2.cloned.1.call-update) | async-done | bytes 1048592 | tf_op jit(solution)/shard_map/all_gather | solution.py:147
  250.5 4.2 %fusion.96 = (bf16[1,2048,128]{1,0,2:T(2,128)(2,1)}, bf16[1,2048,128]{1,0,2:T(2,128)(2,1)S(1)}) fusion(bf16[2,2048,128]{1,0,2:T(2,128)(2,1)} %all-gather.2.cloned.1.call-done), kind=kLoop, calls=%fused_computation.165 | loop fusion | bytes 2097152 | tf_op jit(solution)/shard_map/slice | solution.py:101
  254.7 0.8 copy.158
  255.6 0.4 fusion.29
  256.0 2.4 copy.156
  258.4 0.4 fusion.22
  258.9 0.4 fusion.27
  259.3 0.4 fusion.21
  259.8 1.5 pad_maximum_fusion.1
  261.8 3.6 %copy.154 = bf16[2,8,256,128]{3,2,1,0:T(8,128)(2,1)} copy(bf16[2,8,256,128]{2,0,3,1:T(2,128)(2,1)} %bitcast.37) | data formatting | bytes 2097152 | tf_op jit(solution)/shard_map/all_to_all | solution.py:141
  265.4 0.4 fusion.37
  265.8 0.4 fusion.18
  266.3 0.4 fusion.35
  266.7 0.4 fusion.17
  267.2 0.5 maximum_bitcast_fusion.6
  267.7 0.5 bitcast_convert_fusion
  268.2 4.0 %fusion.9 = f32[2,1,256,4096]{3,2,1,0:T(8,128)} fusion(f32[2,1,256,2048]{3,2,0,1:T(8,128)S(1)} %bitcast_convert_fusion, f32[2,1,256,2048]{3,2,0,1:T(8,128)S(1)} %maximum_bitcast_fusion.6, pred[]{:T(512)S(6)} %eq.19), kind=kLoop, calls=%fused_computation.21 | loop fusion | flops 8388608 | bytes 16777216
  (48 shorter events, 3.7 us)
Async XLA Ops:
  7.2 11.8 %copy-start.1 = (f32[2,2049]{1,0:T(2,128)S(1)}, f32[2,2049]{1,0:T(2,128)}, u32[]{:S(2)}) copy-start(f32[2,2049]{1,0:T(2,128)} %param.4) | copy-start | bytes 49180
  7.2 12.2 %copy-start.2 = (s32[2,8]{1,0:T(2,128)S(1)}, s32[2,8]{1,0:T(2,128)}, u32[]{:S(2)}) copy-start(s32[2,8]{1,0:T(2,128)} %param.5) | copy-start | bytes 196
  11.0 33.0 %all-to-all-start = ((bf16[2,2048,128]{2,0,1:T(2,128)(2,1)}), bf16[2,2048,128]{2,0,1:T(2,128)(2,1)S(1)}, u32[]{:S(2)}, u32[]{:S(2)}) async-start(bf16[2,2048,128]{2,0,1:T(2,128)(2,1)} %bitcast), calls=%async_computation | async-start | bytes 2097152 | tf_op jit(solution)/shard_map/all_to_all | solution.py:126
  18.3 232.3 %all-gather.2.cloned.1.call-start = ((), (), s32[]{:S(2)}) async-start(), calls=%async_computation.2 | async-start | bytes 1179648 | tf_op jit(solution)/shard_map/all_gather | solution.py:147
  200.2 4.3 %collective-permute-start = (bf16[2,256,128]{1,0,2:T(2,128)(2,1)}, bf16[2,256,128]{1,0,2:T(2,128)(2,1)S(1)}, u32[]{:S(2)}, u32[]{:S(2)}) collective-permute-start(bf16[2,256,128]{1,0,2:T(2,128)(2,1)} %fusion.39), channel_id=1, source_target_pairs={{0,1},{1,0},{2,3},{3,2},{4,5},{5,4},{6,7},{7,6},{8,9},{9,8},{10,11... | collective-permute-start | bytes 393224 | tf_op jit(solution)/shard_map/ppermute | solution.py:15
  200.3 61.4 %all-to-all-start.1 = ((bf16[2,256,1024]{1,0,2:T(2,128)(2,1)}), bf16[2,256,1024]{1,0,2:T(2,128)(2,1)}, u32[]{:S(2)}, u32[]{:S(2)}) async-start(bf16[2,256,1024]{1,0,2:T(2,128)(2,1)} %pad_maximum_fusion.2), calls=%async_computation.1 | async-start | bytes 2097152 | tf_op jit(solution)/shard_map/all_to_all | solution.py:141
  259.3 2.0 copy-start
  261.3 6.4 %collective-permute-start.1 = (bf16[2,256,2048]{2,1,0:T(8,128)(2,1)}, bf16[2,256,2048]{2,1,0:T(8,128)(2,1)S(1)}, u32[]{:S(2)}, u32[]{:S(2)}) collective-permute-start(bf16[2,256,2048]{2,1,0:T(8,128)(2,1)} %pad_maximum_fusion.1), channel_id=1, source_target_pairs={{0,1},{1,0},{2,3},{3,2},{4,5},{5,4},{6,7},{7,6},{8,9},{9,8},{10,11... | collective-permute-start | bytes 6291464 | tf_op jit(solution)/shard_map/ppermute | solution.py:15
Sparse Core Ops, SparseCore 0:
  200.4 50.1 all-gather.1
where the time goes:
time: 284 us; the launch traced here: 279 us
  waiting for transfers between devices  67.9 us (24%)
  other arithmetic  66.6 us (23%)
  matrix products  62.1 us (22%)
  local copies, waits for them, and re-layouts  56.4 us (20%)
  between operations  14.6 us (5%)
  starting transfers between devices  11.6 us (4%)
    all_gather x1, waiting for transfers between devices, on_device(): piece = lax.all_gather(snapshots, 'range', axis=1, tiled=True)  45.5 us
    dot_general x3, matrix products, left_section(): jnp.einsum('ckn,...nr->...ckr', stacked, values, precision=lax.Precision....  33.8 us
    dot_general x3, matrix products, right_section(): jnp.einsum('...km,mj->...kj', values, block, precision=lax.Precision.HIGH...  24.8 us
    sub x4, other arithmetic, merged_times(): first_re * second_re - first_im * second_im  22.9 us
    all_to_all x1, waiting for transfers between devices, on_device(): lax.all_to_all(local, 'range', split_axis=1, concat_axis=2, tiled=True)  22.4 us
    squeeze x2, local copies, waits for them, and re-layouts, on_device(): merged = jnp.concatenate([frames[0], frames[1]], axis=-1)  18.2 us
    another operation x3, other arithmetic  16.1 us
    sub x1, other arithmetic, left_section(): real_part = mixed[..., 0, :, :half] - mixed[..., 1, :, half:]  11.4 us
  transfers between devices with their start and end apart: 5, of which 2 were waited for; matrix products, arithmetic and copies ran while one was open for 7% of the time, Pallas kernels for 0%

commit v1 on v0

v1 whole, which is shorter than its diff:
```python
from functools import partial

import jax
import jax.numpy as jnp
from jax import lax
from jax.experimental import pallas as pl
from jax.experimental.pallas import tpu as pltpu
from jax.sharding import PartitionSpec as P

TRAIN = 128
BLOCK = 128


def train_cells(gates, count):
    starts = gates[0]
    widths = gates[1]
    ends = jnp.cumsum(widths)
    places = jnp.arange(count, dtype=jnp.int32)
    which = jnp.sum((ends[None, :] <= places[:, None]).astype(jnp.int32), axis=1)
    onehot = jnp.arange(gates.shape[1], dtype=jnp.int32)[None, :] == which[:, None]
    offset = jnp.sum(jnp.where(onehot, (starts - (ends - widths))[None, :], 0), axis=1)
    return offset + places


def toeplitz_blocks(chirp, lags):
    taps = chirp.shape[1]
    length = BLOCK * lags + BLOCK - 1
    pad_after = max(0, length - (BLOCK - 1) - taps)
    u = jnp.pad(chirp, ((0, 0), (BLOCK - 1, pad_after)))[:, :length]
    tiled = jnp.tile(u, (1, BLOCK + 1))[:, : BLOCK * (length + 1)]
    windows = tiled.reshape(2, BLOCK, length + 1)[:, :, : BLOCK * lags]
    full = windows[:, ::-1, :]
    blocks = full.reshape(2, BLOCK, lags, BLOCK).transpose(0, 2, 1, 3)
    t_re = blocks[0]
    t_im = blocks[1]
    top = jnp.concatenate([t_re, t_im], axis=2)
    bottom = jnp.concatenate([-t_im, t_re], axis=2)
    w = jnp.concatenate([top, bottom], axis=1)
    hi = w.astype(jnp.bfloat16)
    lo = (w - hi.astype(jnp.float32)).astype(jnp.bfloat16)
    return jnp.concatenate([hi, lo], axis=2)


def conv_kernel(x_ref, w_ref, o_ref, *, lags):
    d = pl.program_id(0)
    rows = x_ref.shape[0]
    width = 2 * BLOCK

    def body(j, acc):
        start = pl.multiple_of((d - j) * width, width)
        xs = x_ref[:, pl.ds(start, width)]
        return acc + jnp.dot(xs, w_ref[j], preferred_element_type=jnp.float32)

    count = jnp.minimum(d, lags - 1) + 1
    acc = lax.fori_loop(0, count, body, jnp.zeros((rows, 2 * width), jnp.float32))
    o_ref[...] = (acc[:, :width] + acc[:, width:]).astype(o_ref.dtype)


def causal_filter(x, w):
    rows, total = x.shape
    lags = w.shape[0]
    nblocks = total // (2 * BLOCK)
    work = rows * (2 * BLOCK) * (4 * BLOCK) * 2 * nblocks * min(lags, nblocks)
    return pl.pallas_call(
        partial(conv_kernel, lags=lags),
        out_shape=jax.ShapeDtypeStruct((rows, total), jnp.bfloat16),
        grid=(nblocks,),
        in_specs=[
            pl.BlockSpec((rows, total), lambda d: (0, 0)),
            pl.BlockSpec(w.shape, lambda d: (0, 0, 0)),
        ],
        out_specs=pl.BlockSpec((rows, 2 * BLOCK), lambda d: (0, d)),
        compiler_params=pltpu.CompilerParams(vmem_limit_bytes=48 * 1024 * 1024),
        cost_estimate=pl.CostEstimate(
            flops=work, transcendentals=0, bytes_accessed=2 * x.size * 2 + w.size * 2
        ),
    )(x, w)


def on_device(echoes, chirp, gates):
    chans = echoes.shape[1]
    pulses = echoes.shape[2]
    cells_dev = echoes.shape[3]
    taps = chirp.shape[1]
    ranks = lax.axis_size("range")
    range_len = cells_dev * ranks
    nblocks = range_len // BLOCK
    per_dev_blocks = cells_dev // BLOCK
    lags = min((taps - 1 + BLOCK - 1) // BLOCK + 1, nblocks)
    series_total = chans * pulses
    series_dev = series_total // ranks

    w = toeplitz_blocks(chirp, lags)

    local = echoes.reshape(2, series_total, per_dev_blocks, BLOCK).transpose(1, 2, 0, 3)
    series_all = lax.all_to_all(local, "range", split_axis=0, concat_axis=1, tiled=True)
    x = series_all.reshape(series_dev, nblocks * 2 * BLOCK)
    y = causal_filter(x, w)
    y4 = y.reshape(series_dev, nblocks, 2, BLOCK)

    returned = lax.all_to_all(y4, "range", split_axis=1, concat_axis=0, tiled=True)
    compressed = returned.reshape(chans, pulses, per_dev_blocks, 2, BLOCK)
    compressed = compressed.transpose(3, 0, 1, 2, 4).reshape(2, chans, pulses, cells_dev)

    cells = train_cells(gates, TRAIN)
    by_cell = y4.transpose(1, 3, 0, 2).reshape(range_len, series_dev, 2)
    picked = jnp.take(by_cell, cells, axis=0)
    snap = picked.transpose(1, 2, 0).reshape(series_dev, 2 * TRAIN)

    half = lax.all_gather(snap, "range", axis=0, tiled=True)
    every = lax.all_gather(half, "chan", axis=0, tiled=True)

    snap_re = snap[:, :TRAIN]
    snap_im = snap[:, TRAIN:]
    left = jnp.concatenate([snap, jnp.concatenate([snap_im, -snap_re], axis=1)], axis=0)
    gram = lax.dot_general(
        left, every, (((1,), (1,)), ((), ())), preferred_element_type=jnp.float32
    )
    covariance = (gram * (1.0 / TRAIN)).reshape(2, 1, series_dev, -1)
    return (compressed, covariance)


def solution(mesh):
    placed = (P("groups", "chan", None, "range"), P(), P("groups", None))
    return jax.shard_map(
        on_device,
        mesh=mesh,
        in_specs=placed,
        out_specs=(P("groups", "chan", None, "range"), P("groups", "chan", "range", None)),
        check_vma=False,
    )
```

time: 284 us -> 150 us (0.53); the launches traced: 279 us -> 149 us
  other arithmetic: 66.6 us -> 1.11 us
  matrix products: 62.1 us -> 6.27 us
  local copies, waits for them, and re-layouts: 56.4 us -> 27 us
  waiting for transfers between devices: 67.9 us -> 79.1 us
  Pallas kernels: 0 us -> 10.7 us
    dot_general x14 -> x1, matrix products: 62.1 us -> 6.27 us  [on_device(): lax.dot_general(left, every, (((1,), (1,)), ((), ())), preferred_element_...]
    sub x5 -> x0, other arithmetic: 34.3 us -> none  [the longest x4 22.9 us: merged_times(): first_re * second_re - first_im * second_im]
    another operation x7 -> x1, other arithmetic: 21.1 us -> 0.18 us
    squeeze x4 -> x1, local copies, waits for them, and re-layouts: 18.4 us -> 0.07 us  [toeplitz_blocks(): t_im = blocks[1]]
    all_to_all x2, waiting for transfers between devices: 22.4 us -> 40.4 us  [the longest x1 25.5 us: on_device(): lax.all_to_all(y4, 'range', split_axis=1, concat_axis=0, tiled=True)]
    pallas_call x0 -> x1, Pallas kernels: none -> 10.7 us  [causal_filter(): pl.pallas_call(partial(conv_kernel, lags=lags), out_shape=jax.ShapeDtypeS...]
    reshape x1 -> x8, local copies, waits for them, and re-layouts: 0.01 us -> 10.2 us  [the longest x3 4.61 us: on_device(): y4 = y.reshape(series_dev, nblocks, 2, BLOCK)]
    slice x12 -> x3, local copies, waits for them, and re-layouts: 9.22 us -> 0.32 us  [the longest x1 0.13 us: toeplitz_blocks(): tiled = jnp.tile(u, (1, BLOCK + 1))[:, :BLOCK * (length + 1)]]
  transfers between devices with their start and end apart: 5 -> 4, of which waited for: 2 -> 3; matrix products, arithmetic and copies ran while one was open for 7% -> 9% of each run, Pallas kernels for 0% -> 0%
where the time goes in v1:
time: 150 us; the launch traced here: 149 us
  waiting for transfers between devices  79.1 us (53%)
  local copies, waits for them, and re-layouts  27 us (18%)
  between operations  14.3 us (10%)
  starting transfers between devices  10.9 us (7%)
  Pallas kernels  10.7 us (7%)
  matrix products  6.27 us (4%)
    all_gather x1, waiting for transfers between devices, on_device(): half = lax.all_gather(snap, 'range', axis=0, tiled=True)  38.7 us
    all_to_all x1, waiting for transfers between devices, on_device(): lax.all_to_all(y4, 'range', split_axis=1, concat_axis=0, tiled=True)  25.5 us
    all_to_all x1, waiting for transfers between devices, on_device(): lax.all_to_all(local, 'range', split_axis=0, concat_axis=1, tiled=True)  14.9 us
    pallas_call x1, Pallas kernels, causal_filter(): pl.pallas_call(partial(conv_kernel, lags=lags), out_shape=jax.ShapeDtypeS...  10.7 us
    all_to_all x1, starting transfers between devices, on_device(): lax.all_to_all(local, 'range', split_axis=0, concat_axis=1, tiled=True)  7.25 us
    dot_general x1, matrix products, on_device(): lax.dot_general(left, every, (((1,), (1,)), ((), ())), preferred_element_...  6.27 us
    rev x1, local copies, waits for them, and re-layouts, toeplitz_blocks(): full = windows[:, ::-1, :]  5.85 us
    unnamed x11, local copies, waits for them, and re-layouts  5.21 us
  transfers between devices with their start and end apart: 4, of which 3 were waited for; matrix products, arithmetic and copies ran while one was open for 9% of the time, Pallas kernels for 0%

profile of v1, /device:TPU:0, one launch (start us, length us, event | category | flops | bytes accessed | tf_op | source)
XLA Modules:
  0.0 149.4 jit_solution(1215066634217724559)
XLA Ops:
  7.2 0.0 copy-start.3
  7.2 0.0 copy-start.2
  7.2 3.8 %copy.32 = bf16[2,256,8,128]{3,0,2,1:T(2,128)(2,1)} copy(bf16[2,256,8,128]{3,2,1,0:T(8,128)(2,1)} %param.3) | data formatting | bytes 2097152 | tf_op args[0]
  11.0 7.3 %all-to-all-start = ((bf16[2048,1,2,128]{3,2,1,0:T(2,128)(2,1)}), bf16[2048,1,2,128]{3,2,1,0:T(2,128)(2,1)S(1)}, u32[]{:S(2)}, u32[]{:S(2)}) async-start(bf16[2048,1,2,128]{3,2,1,0:T(2,128)(2,1)} %bitcast.1), calls=%async_computation | async-start | bytes 2097152 | tf_op jit(solution)/shard_map/all_to_all | solution.py:96
  18.3 0.0 all-gather.3.cloned.1.call-start
  18.3 0.0 copy-done.3
  18.3 0.2 reduce-window.4
  18.5 0.1 convert_reduce_fusion
  18.6 0.0 copy-done.2
  18.6 0.1 pad_slice_fusion
  18.7 0.1 tile.4
  18.8 1.6 %tile.10 = f32[2,148479]{1,0:T(2,128)S(1)} reshape(f32[2,129,1151]{2,1,0:T(8,128)S(1)} %tile.4) | data formatting | bytes 2375664 | tf_op jit(solution)/shard_map/tile | solution.py:30
  20.3 0.1 slice.38
  20.5 0.1 copy.47
  20.6 0.1 slice.39
  20.7 0.3 copy.43
  21.0 5.8 %rev.3 = f32[2,128,1024]{1,2,0:T(8,128)} reverse(f32[2,128,1024]{1,2,0:T(8,128)S(1)} %copy.43), dimensions={1} | reverse | bytes 2097152 | tf_op jit(solution)/shard_map/rev | solution.py:32
  26.9 1.6 %copy.36 = f32[2,128,8,128]{3,1,2,0:T(8,128)S(1)} copy(f32[2,128,8,128]{1,3,2,0:T(8,128)} %bitcast.63) | data formatting | bytes 2097152 | tf_op jit(solution)/shard_map/reshape | solution.py:33
  28.5 0.1 select_reduce_fusion
  28.6 0.1 slice_bitcast_fusion
  28.7 0.1 subtract_convert_fusion
  28.8 0.1 fusion
  29.0 0.2 pad_maximum_fusion.w_ref
  29.2 14.9 %all-to-all-done = bf16[2048,1,2,128]{3,2,1,0:T(2,128)(2,1)S(1)} async-done(((bf16[2048,1,2,128]{3,2,1,0:T(2,128)(2,1)}), bf16[2048,1,2,128]{3,2,1,0:T(2,128)(2,1)S(1)}, u32[]{:S(2)}, u32[]{:S(2)}) %all-to-all-start) | async-done | bytes 1048608 | tf_op jit(solution)/shard_map/all_to_all | solution.py:96
  44.0 0.1 copy.33
  44.2 2.0 %copy.34 = bf16[256,8,1,2,128]{4,3,1,0,2:T(2,128)(2,1)} copy(bf16[256,8,1,2,128]{4,0,1,3,2:T(8,128)(2,1)S(1)} %bitcast.64) | data formatting | bytes 2097152 | tf_op jit(solution)/shard_map/all_to_all | solution.py:96
  46.2 1.8 %reshape.78.x_ref = bf16[256,2048]{1,0:T(8,128)(2,1)S(1)} reshape(bf16[256,8,1,2,128]{4,3,1,0,2:T(2,128)(2,1)} %copy.34) | data formatting | bytes 2097152 | tf_op jit(solution)/shard_map/reshape | solution.py:97
  48.1 10.7 %shard_map.50 = bf16[256,2048]{1,0:T(8,128)(2,1)S(1)} custom-call(bf16[256,2048]{1,0:T(8,128)(2,1)S(1)} %reshape.78.x_ref, bf16[8,256,512]{2,1,0:T(8,128)(2,1)S(1)} %pad_maximum_fusion.w_ref), custom_call_target="tpu_custom_call" | custom-call | flops 4294967296 | bytes 4194304 | tf_op jit(solution)/shard_map/pallas_call | solution.py:64
  58.8 0.0 copy-start
  58.8 1.0 copy-done
  59.8 1.8 %reshape.81 = bf16[256,8,2,128]{3,2,1,0:T(2,128)(2,1)S(1)} reshape(bf16[256,2048]{1,0:T(8,128)(2,1)} %copy-done) | data formatting | bytes 2097152 | tf_op jit(solution)/shard_map/reshape | solution.py:99
  61.6 1.1 copy.39
  62.6 1.1 copy.40
  63.7 0.9 gather_fusion
  64.6 0.2 fusion.6
  64.8 0.7 copy.41
  65.5 0.0 all-gather.3.cloned.1.call-update
  65.5 0.0 all-gather.5.cloned.1.call-start
  65.6 38.7 %all-gather.3.cloned.1.call-done = bf16[2048,256]{0,1:T(8,128)(2,1)} async-done(((bf16[256,256]{0,1:T(8,128)(2,1)}), bf16[2048,256]{0,1:T(8,128)(2,1)}) %all-gather.3.cloned.1.call-update) | async-done | bytes 1048592 | tf_op jit(solution)/shard_map/all_gather | solution.py:110
  104.2 0.0 all-gather.5.cloned.1.call-update
  104.3 0.0 copy-start.1
  104.3 1.8 %copy.37 = bf16[256,8,2,128]{3,2,0,1:T(2,128)(2,1)} copy(bf16[256,8,2,128]{3,2,1,0:T(2,128)(2,1)S(1)} %reshape.81) | data formatting | bytes 2097152 | tf_op jit(solution)/shard_map/reshape | solution.py:99
  106.0 3.6 %all-to-all-start.1 = ((bf16[256,8,2,128]{3,2,0,1:T(2,128)(2,1)}), bf16[256,8,2,128]{3,2,0,1:T(2,128)(2,1)S(1)}, u32[]{:S(2)}, u32[]{:S(2)}) async-start(bf16[256,8,2,128]{3,2,0,1:T(2,128)(2,1)} %copy.37), calls=%async_computation.1 | async-start | bytes 2097152 | tf_op jit(solution)/shard_map/all_to_all | solution.py:101
  109.6 0.0 copy-done.1
  109.6 25.5 %all-to-all-done.1 = bf16[256,8,2,128]{3,2,0,1:T(2,128)(2,1)S(1)} async-done(((bf16[256,8,2,128]{3,2,0,1:T(2,128)(2,1)}), bf16[256,8,2,128]{3,2,0,1:T(2,128)(2,1)S(1)}, u32[]{:S(2)}, u32[]{:S(2)}) %all-to-all-start.1) | async-done | bytes 1048608 | tf_op jit(solution)/shard_map/all_to_all | solution.py:101
  135.1 1.1 copy.48
  136.2 0.0 all-gather.5.cloned.1.call-done
  136.2 6.3 %convolution_multiply_fusion = f32[512,4096]{1,0:T(8,128)} fusion(bf16[4096,256]{0,1:T(8,128)(2,1)} %all-gather.5.cloned.1.call-done, bf16[256,128]{0,1:T(8,128)(2,1)S(1)} %get-tuple-element.15, bf16[256,128]{0,1:T(8,128)(2,1)S(1)} %get-tuple-element.14, bf16[256,256]{0,1:T(8,128)(2,1)S(1)} %bitcast.68), kind=kOutput, calls=%fused_computation.1 | convolution fusion | flops 1076625408 | bytes 10747904 | tf_op jit(solution)/shard_map/dot_general | solution.py:116
  (7 shorter events, 0.1 us)
Async XLA Ops:
  7.2 11.1 %copy-start.3 = (s32[2,8]{1,0:T(2,128)S(1)}, s32[2,8]{1,0:T(2,128)}, u32[]{:S(2)}) copy-start(s32[2,8]{1,0:T(2,128)} %param.5) | copy-start | bytes 196
  7.2 11.4 %copy-start.2 = (f32[2,2049]{1,0:T(2,128)S(1)}, f32[2,2049]{1,0:T(2,128)}, u32[]{:S(2)}) copy-start(f32[2,2049]{1,0:T(2,128)} %param.4) | copy-start | bytes 49180
  11.0 33.0 %all-to-all-start = ((bf16[2048,1,2,128]{3,2,1,0:T(2,128)(2,1)}), bf16[2048,1,2,128]{3,2,1,0:T(2,128)(2,1)S(1)}, u32[]{:S(2)}, u32[]{:S(2)}) async-start(bf16[2048,1,2,128]{3,2,1,0:T(2,128)(2,1)} %bitcast.1), calls=%async_computation | async-start | bytes 2097152 | tf_op jit(solution)/shard_map/all_to_all | solution.py:96
  18.3 86.0 %all-gather.3.cloned.1.call-start = ((), (), s32[]{:S(2)}) async-start(), calls=%async_computation.2 | async-start | bytes 1179648 | tf_op jit(solution)/shard_map/all_gather | solution.py:110
  58.8 1.0 copy-start
  65.5 70.7 %all-gather.5.cloned.1.call-start = ((), (), s32[]{:S(2)}) async-start(), calls=%async_computation.3 | async-start | bytes 3145728 | tf_op jit(solution)/shard_map/all_gather | solution.py:111
  104.3 5.4 %copy-start.1 = (bf16[256,2,128]{0,2,1:T(8,128)(2,1)S(1)}, bf16[256,2,128]{0,2,1:T(8,128)(2,1)}, u32[]{:S(2)}) copy-start(bf16[256,2,128]{0,2,1:T(8,128)(2,1)} %copy.41) | copy-start | bytes 393220
  106.0 29.1 %all-to-all-start.1 = ((bf16[256,8,2,128]{3,2,0,1:T(2,128)(2,1)}), bf16[256,8,2,128]{3,2,0,1:T(2,128)(2,1)S(1)}, u32[]{:S(2)}, u32[]{:S(2)}) async-start(bf16[256,8,2,128]{3,2,0,1:T(2,128)(2,1)} %copy.37), calls=%async_computation.1 | async-start | bytes 2097152 | tf_op jit(solution)/shard_map/all_to_all | solution.py:101
Sparse Core Ops, SparseCore 0:
  65.6 38.5 all-gather.2
  105.8 9.4 all-gather.4

commit v2 on v1

--- a/solution.py
+++ b/solution.py
@@ -98,16 +98,20 @@
     y = causal_filter(x, w)
     y4 = y.reshape(series_dev, nblocks, 2, BLOCK)
 
-    returned = lax.all_to_all(y4, "range", split_axis=1, concat_axis=0, tiled=True)
-    compressed = returned.reshape(chans, pulses, per_dev_blocks, 2, BLOCK)
-    compressed = compressed.transpose(3, 0, 1, 2, 4).reshape(2, chans, pulses, cells_dev)
-
     cells = train_cells(gates, TRAIN)
     by_cell = y4.transpose(1, 3, 0, 2).reshape(range_len, series_dev, 2)
     picked = jnp.take(by_cell, cells, axis=0)
     snap = picked.transpose(1, 2, 0).reshape(series_dev, 2 * TRAIN)
 
-    half = lax.all_gather(snap, "range", axis=0, tiled=True)
+    own_width = per_dev_blocks * 2 * BLOCK
+    spread = jnp.broadcast_to(snap[:, None, :], (series_dev, ranks, 2 * TRAIN))
+    both = jnp.concatenate([y.reshape(series_dev, ranks, own_width), spread], axis=2)
+    arrived = lax.all_to_all(both, "range", split_axis=1, concat_axis=0, tiled=True)
+    returned = arrived[:, 0, :own_width]
+    half = arrived[:, 0, own_width:]
+    compressed = returned.reshape(chans, pulses, per_dev_blocks, 2, BLOCK)
+    compressed = compressed.transpose(3, 0, 1, 2, 4).reshape(2, chans, pulses, cells_dev)
+
     every = lax.all_gather(half, "chan", axis=0, tiled=True)
 
     snap_re = snap[:, :TRAIN]

time: 150 us -> 143 us (0.953)
  blocking collectives: 0 us -> 51.8 us
  waiting for transfers between devices: 79.1 us -> 29.4 us
  local copies, waits for them, and re-layouts: 27 us -> 21.3 us
  starting transfers between devices: 10.9 us -> 7.29 us
    all_to_all x0 -> x1, blocking collectives: none -> 51.8 us  [on_device(): lax.all_to_all(both, 'range', split_axis=1, concat_axis=0, tiled=True)]
    all_gather x1 -> x0, waiting for transfers between devices: 38.7 us -> none  [on_device(): half = lax.all_gather(snap, 'range', axis=0, tiled=True)]
    all_to_all x1 -> x0, waiting for transfers between devices: 25.5 us -> none  [on_device(): lax.all_to_all(y4, 'range', split_axis=1, concat_axis=0, tiled=True)]
    all_gather x1, waiting for transfers between devices: 0.01 us -> 8.75 us  [on_device(): every = lax.all_gather(half, 'chan', axis=0, tiled=True)]
    all_to_all x1, waiting for transfers between devices: 14.9 us -> 20.6 us  [on_device(): lax.all_to_all(local, 'range', split_axis=0, concat_axis=1, tiled=True)]
    rev x1, local copies, waits for them, and re-layouts: 5.85 us -> 1.43 us  [toeplitz_blocks(): full = windows[:, ::-1, :]]
    all_to_all x1 -> x0, starting transfers between devices: 3.56 us -> none  [on_device(): lax.all_to_all(y4, 'range', split_axis=1, concat_axis=0, tiled=True)]
    reshape x3 -> x2, local copies, waits for them, and re-layouts: 4.61 us -> 1.8 us  [on_device(): y4 = y.reshape(series_dev, nblocks, 2, BLOCK)]
  transfers between devices with their start and end apart: 4 -> 2, of which waited for: 3 -> 2; matrix products, arithmetic and copies ran while one was open for 9% -> 4% of each run, Pallas kernels for 0% -> 0%
where the time goes in v2:
time: 143 us; the launch traced here: 142 us
  blocking collectives  51.8 us (36%)
  waiting for transfers between devices  29.4 us (21%)
  local copies, waits for them, and re-layouts  21.3 us (15%)
  between operations  14.3 us (10%)
  Pallas kernels  10.7 us (7%)
  starting transfers between devices  7.29 us (5%)
  matrix products  6.3 us (4%)
    all_to_all x1, blocking collectives, on_device(): lax.all_to_all(both, 'range', split_axis=1, concat_axis=0, tiled=True)  51.8 us
    all_to_all x1, waiting for transfers between devices, on_device(): lax.all_to_all(local, 'range', split_axis=0, concat_axis=1, tiled=True)  20.6 us
    pallas_call x1, Pallas kernels, causal_filter(): pl.pallas_call(partial(conv_kernel, lags=lags), out_shape=jax.ShapeDtypeS...  10.7 us
    all_gather x1, waiting for transfers between devices, on_device(): every = lax.all_gather(half, 'chan', axis=0, tiled=True)  8.75 us
    unnamed x12, local copies, waits for them, and re-layouts  7.28 us
    all_to_all x1, starting transfers between devices, on_device(): lax.all_to_all(local, 'range', split_axis=0, concat_axis=1, tiled=True)  7.25 us
    dot_general x1, matrix products, on_device(): lax.dot_general(left, every, (((1,), (1,)), ((), ())), preferred_element_...  6.3 us
  transfers between devices with their start and end apart: 2, of which 2 were waited for; matrix products, arithmetic and copies ran while one was open for 4% of the time, Pallas kernels for 0%

profile of v2, /device:TPU:0, one launch (start us, length us, event | category | flops | bytes accessed | tf_op | source)
XLA Modules:
  0.0 142.3 jit_solution(8375970480125497359)
XLA Ops:
  7.2 0.0 copy-start.3
  7.2 0.0 copy-start.2
  7.2 3.8 %copy.36 = bf16[2,256,8,128]{3,0,2,1:T(2,128)(2,1)} copy(bf16[2,256,8,128]{3,2,1,0:T(8,128)(2,1)} %param.3) | data formatting | bytes 2097152 | tf_op args[0]
  11.0 7.3 %all-to-all-start = ((bf16[2048,1,2,128]{3,2,1,0:T(2,128)(2,1)}), bf16[2048,1,2,128]{3,2,1,0:T(2,128)(2,1)}, u32[]{:S(2)}, u32[]{:S(2)}) async-start(bf16[2048,1,2,128]{3,2,1,0:T(2,128)(2,1)} %bitcast.1), calls=%async_computation | async-start | bytes 2097152 | tf_op jit(solution)/shard_map/all_to_all | solution.py:96
  18.3 0.0 all-gather.3.cloned.1.call-start
  18.3 0.0 copy-done.3
  18.3 0.2 reduce-window.4
  18.5 0.1 convert_reduce_fusion
  18.6 0.0 copy-done.2
  18.6 0.1 pad_slice_fusion
  18.7 0.1 tile.4
  18.8 1.6 %tile.10 = f32[2,148479]{1,0:T(2,128)S(1)} reshape(f32[2,129,1151]{2,1,0:T(8,128)S(1)} %tile.4) | data formatting | bytes 2375664 | tf_op jit(solution)/shard_map/tile | solution.py:30
  20.3 0.1 slice.46
  20.5 0.1 copy.53
  20.6 0.1 slice.47
  20.7 0.3 copy.48
  21.0 1.4 %rev.3 = f32[2,128,1024]{1,2,0:T(8,128)S(1)} reverse(f32[2,128,1024]{1,2,0:T(8,128)S(1)} %copy.48), dimensions={1} | reverse | bytes 2097152 | tf_op jit(solution)/shard_map/rev | solution.py:32
  22.5 0.3 copy.40
  22.8 0.1 select_reduce_fusion
  23.0 0.1 slice_bitcast_fusion.1
  23.1 0.1 subtract_convert_fusion
  23.2 0.1 fusion.1
  23.3 0.2 pad_maximum_fusion.w_ref
  23.5 20.6 %all-to-all-done = bf16[2048,1,2,128]{3,2,1,0:T(2,128)(2,1)} async-done(((bf16[2048,1,2,128]{3,2,1,0:T(2,128)(2,1)}), bf16[2048,1,2,128]{3,2,1,0:T(2,128)(2,1)}, u32[]{:S(2)}, u32[]{:S(2)}) %all-to-all-start) | async-done | bytes 1048608 | tf_op jit(solution)/shard_map/all_to_all | solution.py:96
  44.1 1.4 copy.37
  45.5 1.1 copy.38
  46.6 1.6 %reshape.76.x_ref = bf16[256,2048]{1,0:T(8,128)(2,1)} reshape(bf16[256,8,1,2,128]{4,3,1,0,2:T(2,128)(2,1)S(1)} %copy.38) | data formatting | bytes 2097152 | tf_op jit(solution)/shard_map/reshape | solution.py:97
  48.2 0.0 copy-start
  48.2 1.2 copy-done
  49.4 10.7 %shard_map.50 = bf16[256,2048]{1,0:T(8,128)(2,1)S(1)} custom-call(bf16[256,2048]{1,0:T(8,128)(2,1)S(1)} %copy-done, bf16[8,256,512]{2,1,0:T(8,128)(2,1)S(1)} %pad_maximum_fusion.w_ref), custom_call_target="tpu_custom_call" | custom-call | flops 4294967296 | bytes 4194304 | tf_op jit(solution)/shard_map/pallas_call | solution.py:64
  60.1 0.8 reshape.82
  60.9 1.0 copy.54
  61.9 1.0 copy.41
  63.0 1.1 copy.42
  64.1 0.9 gather_fusion
  64.9 0.0 copy-start.1
  64.9 0.2 fusion.7
  65.2 0.1 copy.44
  65.3 0.1 broadcast_in_dim.42
  65.4 0.8 copy-done.1
  66.2 0.2 pad_maximum_fusion.1
  66.3 51.8 %all_to_all.33 = bf16[256,8,512]{2,0,1:T(8,128)(2,1)S(1)} all-to-all(bf16[256,8,512]{2,0,1:T(8,128)(2,1)S(1)} %pad_maximum_fusion.1), channel_id=1, replica_groups=mesh['groups'=2,'range'=8,'chan'=2] {'range'}, dimensions={1} | all-to-all | bytes 4194304 | tf_op jit(solution)/shard_map/all_to_all | solution.py:109
  118.1 1.2 fusion.13
  119.3 0.0 all-gather.3.cloned.1.call-update
  119.4 1.0 copy.46
  120.4 8.7 %all-gather.3.cloned.1.call-done = bf16[4096,1,256]{2,0,1:T(8,128)(2,1)} async-done(((bf16[2048,1,256]{2,0,1:T(8,128)(2,1)}), bf16[4096,1,256]{2,0,1:T(8,128)(2,1)}) %all-gather.3.cloned.1.call-update) | async-done | bytes 2097168 | tf_op jit(solution)/shard_map/all_gather | solution.py:115
  129.1 6.3 %convolution_multiply_fusion = f32[512,4096]{1,0:T(8,128)} fusion(bf16[4096,1,256]{2,0,1:T(8,128)(2,1)} %all-gather.3.cloned.1.call-done, bf16[256,128]{0,1:T(8,128)(2,1)S(1)} %get-tuple-element.17, bf16[256,128]{0,1:T(8,128)(2,1)S(1)} %get-tuple-element.16, bf16[256,256]{0,1:T(8,128)(2,1)S(1)} %bitcast.77), kind=kOutput, calls=%fused_computation.1 | convolution fusion | flops 1076625408 | bytes 10747904 | tf_op jit(solution)/shard_map/dot_general | solution.py:120
  (8 shorter events, 0.1 us)
Async XLA Ops:
  7.2 11.1 %copy-start.3 = (s32[2,8]{1,0:T(2,128)S(1)}, s32[2,8]{1,0:T(2,128)}, u32[]{:S(2)}) copy-start(s32[2,8]{1,0:T(2,128)} %param.5) | copy-start | bytes 196
  7.2 11.4 %copy-start.2 = (f32[2,2049]{1,0:T(2,128)S(1)}, f32[2,2049]{1,0:T(2,128)}, u32[]{:S(2)}) copy-start(f32[2,2049]{1,0:T(2,128)} %param.4) | copy-start | bytes 49180
  11.0 33.1 %all-to-all-start = ((bf16[2048,1,2,128]{3,2,1,0:T(2,128)(2,1)}), bf16[2048,1,2,128]{3,2,1,0:T(2,128)(2,1)}, u32[]{:S(2)}, u32[]{:S(2)}) async-start(bf16[2048,1,2,128]{3,2,1,0:T(2,128)(2,1)} %bitcast.1), calls=%async_computation | async-start | bytes 2097152 | tf_op jit(solution)/shard_map/all_to_all | solution.py:96
  18.3 110.9 %all-gather.3.cloned.1.call-start = ((), (), s32[]{:S(2)}) async-start(), calls=%async_computation.2 | async-start | bytes 3145728 | tf_op jit(solution)/shard_map/all_gather | solution.py:115
  48.2 1.2 copy-start
  64.9 1.2 copy-start.1
Sparse Core Ops, SparseCore 0:
  119.5 9.6 all-gather.2

commit v3 on v2

--- a/solution.py
+++ b/solution.py
@@ -43,38 +43,35 @@
 
 def conv_kernel(x_ref, w_ref, o_ref, *, lags):
     d = pl.program_id(0)
-    rows = x_ref.shape[0]
     width = 2 * BLOCK
-
-    def body(j, acc):
-        start = pl.multiple_of((d - j) * width, width)
-        xs = x_ref[:, pl.ds(start, width)]
-        return acc + jnp.dot(xs, w_ref[j], preferred_element_type=jnp.float32)
-
-    count = jnp.minimum(d, lags - 1) + 1
-    acc = lax.fori_loop(0, count, body, jnp.zeros((rows, 2 * width), jnp.float32))
+    start = pl.multiple_of(d * width, width)
+    xs = x_ref[:, pl.ds(start, lags * width)]
+    acc = jnp.dot(xs, w_ref[...], preferred_element_type=jnp.float32)
     o_ref[...] = (acc[:, :width] + acc[:, width:]).astype(o_ref.dtype)
 
 
 def causal_filter(x, w):
     rows, total = x.shape
     lags = w.shape[0]
-    nblocks = total // (2 * BLOCK)
-    work = rows * (2 * BLOCK) * (4 * BLOCK) * 2 * nblocks * min(lags, nblocks)
+    width = 2 * BLOCK
+    nblocks = total // width
+    stacked = w[::-1].reshape(lags * width, 2 * width)
+    padded = jnp.pad(x, ((0, 0), ((lags - 1) * width, 0)))
+    work = rows * lags * width * 2 * width * 2 * nblocks
     return pl.pallas_call(
         partial(conv_kernel, lags=lags),
         out_shape=jax.ShapeDtypeStruct((rows, total), jnp.bfloat16),
         grid=(nblocks,),
         in_specs=[
-            pl.BlockSpec((rows, total), lambda d: (0, 0)),
-            pl.BlockSpec(w.shape, lambda d: (0, 0, 0)),
+            pl.BlockSpec(padded.shape, lambda d: (0, 0)),
+            pl.BlockSpec(stacked.shape, lambda d: (0, 0)),
         ],
-        out_specs=pl.BlockSpec((rows, 2 * BLOCK), lambda d: (0, d)),
+        out_specs=pl.BlockSpec((rows, width), lambda d: (0, d)),
         compiler_params=pltpu.CompilerParams(vmem_limit_bytes=48 * 1024 * 1024),
         cost_estimate=pl.CostEstimate(
             flops=work, transcendentals=0, bytes_accessed=2 * x.size * 2 + w.size * 2
         ),
-    )(x, w)
+    )(padded, stacked)
 
 
 def on_device(echoes, chirp, gates):
@@ -112,7 +109,11 @@
     compressed = returned.reshape(chans, pulses, per_dev_blocks, 2, BLOCK)
     compressed = compressed.transpose(3, 0, 1, 2, 4).reshape(2, chans, pulses, cells_dev)
 
-    every = lax.all_gather(half, "chan", axis=0, tiled=True)
+    partner = lax.ppermute(half, "chan", [(0, 1), (1, 0)])
+    upper = lax.axis_index("chan") == 0
+    every = jnp.concatenate(
+        [jnp.where(upper, half, partner), jnp.where(upper, partner, half)], axis=0
+    )
 
     snap_re = snap[:, :TRAIN]
     snap_im = snap[:, TRAIN:]

time: 143 us -> 116 us (0.81)
  between operations: 14.3 us -> 0.86 us
  waiting for transfers between devices: 29.4 us -> 18.5 us
  Pallas kernels: 10.7 us -> 5.81 us
  local copies, waits for them, and re-layouts: 21.3 us -> 24.2 us
  matrix products: 6.3 us -> 4.71 us
    all_gather x1 -> x0, waiting for transfers between devices: 8.75 us -> none  [on_device(): every = lax.all_gather(half, 'chan', axis=0, tiled=True)]
    pallas_call x1, Pallas kernels: 10.7 us -> 5.81 us  [causal_filter(): pl.pallas_call(partial(conv_kernel, lags=lags), out_shape=jax.ShapeDtypeS...]
    rev x0 -> x2, local copies, waits for them, and re-layouts: none -> 4.33 us  [causal_filter(): stacked = w[::-1].reshape(lags * width, 2 * width)]
    all_to_all x1, waiting for transfers between devices: 20.6 us -> 16.6 us  [on_device(): lax.all_to_all(local, 'range', split_axis=0, concat_axis=1, tiled=True)]
    ppermute x0 -> x1, waiting for transfers between devices: none -> 1.95 us  [on_device(): partner = lax.ppermute(half, 'chan', [(0, 1), (1, 0)])]
    dot_general x1, matrix products: 6.3 us -> 4.71 us  [on_device(): lax.dot_general(left, every, (((1,), (1,)), ((), ())), preferred_element_...]
    unnamed x12 -> x10, local copies, waits for them, and re-layouts: 7.28 us -> 6.05 us
  transfers between devices with their start and end apart: 2 -> 2, of which waited for: 2 -> 2; matrix products, arithmetic and copies ran while one was open for 4% -> 9% of each run, Pallas kernels for 0% -> 0%
where the time goes in v3:
time: 116 us
  blocking collectives  51.8 us (45%)
  local copies, waits for them, and re-layouts  24.2 us (21%)
  waiting for transfers between devices  18.5 us (16%)
  starting transfers between devices  7.26 us (6%)
  Pallas kernels  5.81 us (5%)
  matrix products  4.71 us (4%)
  other arithmetic  2.61 us (2%)
    all_to_all x1, blocking collectives, on_device(): lax.all_to_all(both, 'range', split_axis=1, concat_axis=0, tiled=True)  51.8 us
    all_to_all x1, waiting for transfers between devices, on_device(): lax.all_to_all(local, 'range', split_axis=0, concat_axis=1, tiled=True)  16.6 us
    all_to_all x1, starting transfers between devices, on_device(): lax.all_to_all(local, 'range', split_axis=0, concat_axis=1, tiled=True)  7.25 us
    unnamed x10, local copies, waits for them, and re-layouts  6.05 us
    pallas_call x1, Pallas kernels, causal_filter(): pl.pallas_call(partial(conv_kernel, lags=lags), out_shape=jax.ShapeDtypeS...  5.81 us
    dot_general x1, matrix products, on_device(): lax.dot_general(left, every, (((1,), (1,)), ((), ())), preferred_element_...  4.71 us
    rev x2, local copies, waits for them, and re-layouts, causal_filter(): stacked = w[::-1].reshape(lags * width, 2 * width)  4.33 us
  transfers between devices with their start and end apart: 2, of which 2 were waited for; matrix products, arithmetic and copies ran while one was open for 9% of the time, Pallas kernels for 0%

profile of v3, /device:TPU:0, one launch (start us, length us, event | category | flops | bytes accessed | tf_op | source)
XLA Modules:
  0.0 115.7 jit_solution(6796919349015468749)
XLA Ops:
  0.6 0.0 copy-start.1
  0.6 3.8 %copy.36 = bf16[2,256,8,128]{3,0,2,1:T(2,128)(2,1)} copy(bf16[2,256,8,128]{3,2,1,0:T(8,128)(2,1)} %param.3) | data formatting | bytes 2097152 | tf_op args[0]
  4.5 7.3 %all-to-all-start = ((bf16[2048,1,2,128]{3,2,1,0:T(2,128)(2,1)}), bf16[2048,1,2,128]{3,2,1,0:T(2,128)(2,1)S(1)}, u32[]{:S(2)}, u32[]{:S(2)}) async-start(bf16[2048,1,2,128]{3,2,1,0:T(2,128)(2,1)} %bitcast.1), calls=%async_computation | async-start | bytes 2097152 | tf_op jit(solution)/shard_map/all_to_all | solution.py:93
  11.7 0.0 copy-done.1
  11.7 0.1 pad_slice_fusion
  11.8 0.1 tile.4
  11.9 1.6 %tile.10 = f32[2,148479]{1,0:T(2,128)S(1)} reshape(f32[2,129,1151]{2,1,0:T(8,128)S(1)} %tile.4) | data formatting | bytes 2375664 | tf_op jit(solution)/shard_map/tile | solution.py:30
  13.5 0.1 slice.46
  13.6 0.1 copy.53
  13.7 0.1 slice.47
  13.8 0.3 copy.48
  14.1 1.4 %rev.6 = f32[2,128,1024]{1,2,0:T(8,128)S(1)} reverse(f32[2,128,1024]{1,2,0:T(8,128)S(1)} %copy.48), dimensions={1} | reverse | bytes 2097152 | tf_op jit(solution)/shard_map/rev | solution.py:32
  15.6 0.1 slice_bitcast_fusion.2
  15.7 0.1 subtract_convert_fusion
  15.9 0.1 fusion.3
  16.0 0.1 pad_maximum_fusion
  16.1 1.5 %rev.7 = bf16[8,256,512]{1,2,0:T(8,128)(2,1)} reverse(bf16[8,256,512]{1,2,0:T(8,128)(2,1)S(1)} %pad_maximum_fusion), dimensions={0} | reverse | bytes 4194304 | tf_op jit(solution)/shard_map/rev | solution.py:58
  17.6 0.0 copy-start.2
  17.6 2.9 %copy.40 = bf16[8,256,512]{2,1,0:T(8,128)(2,1)S(1)} copy(bf16[8,256,512]{1,2,0:T(8,128)(2,1)} %rev.7) | data formatting | bytes 4194304 | tf_op jit(solution)/shard_map/rev | solution.py:58
  20.5 0.0 copy-done.2
  20.5 0.2 reduce-window.4
  20.7 0.1 convert_reduce_fusion
  20.8 0.1 select_reduce_fusion
  20.9 16.6 %all-to-all-done = bf16[2048,1,2,128]{3,2,1,0:T(2,128)(2,1)S(1)} async-done(((bf16[2048,1,2,128]{3,2,1,0:T(2,128)(2,1)}), bf16[2048,1,2,128]{3,2,1,0:T(2,128)(2,1)S(1)}, u32[]{:S(2)}, u32[]{:S(2)}) %all-to-all-start) | async-done | bytes 1048608 | tf_op jit(solution)/shard_map/all_to_all | solution.py:93
  37.5 0.1 copy.37
  37.6 2.0 %copy.38 = bf16[256,8,1,2,128]{4,3,1,0,2:T(2,128)(2,1)} copy(bf16[256,8,1,2,128]{4,0,1,3,2:T(8,128)(2,1)S(1)} %bitcast.78) | data formatting | bytes 2097152 | tf_op jit(solution)/shard_map/all_to_all | solution.py:93
  39.7 1.8 %reshape.79 = bf16[256,2048]{1,0:T(8,128)(2,1)S(1)} reshape(bf16[256,8,1,2,128]{4,3,1,0,2:T(2,128)(2,1)} %copy.38) | data formatting | bytes 2097152 | tf_op jit(solution)/shard_map/reshape | solution.py:94
  41.5 0.1 pad.8.x_ref
  41.6 5.8 %shard_map.50 = bf16[256,2048]{1,0:T(8,128)(2,1)S(1)} custom-call(bf16[256,3840]{1,0:T(8,128)(2,1)S(1)} %pad.8.x_ref, bf16[2048,512]{1,0:T(8,128)(2,1)S(1)} %bitcast.70), custom_call_target="tpu_custom_call" | custom-call | flops 4294967296 | bytes 4194304 | tf_op jit(solution)/shard_map/pallas_call | solution.py:61
  47.5 0.8 reshape.86
  48.2 1.0 copy.54
  49.3 1.0 copy.41
  50.3 1.1 copy.42
  51.4 0.9 gather_fusion
  52.3 0.0 copy-start
  52.3 0.2 fusion.9
  52.5 0.1 copy.44
  52.7 0.1 broadcast_in_dim.42
  52.7 0.8 copy-done
  53.5 0.2 pad_maximum_fusion.1
  53.7 51.8 %all_to_all.33 = bf16[256,8,512]{2,0,1:T(8,128)(2,1)S(1)} all-to-all(bf16[256,8,512]{2,0,1:T(8,128)(2,1)S(1)} %pad_maximum_fusion.1), channel_id=1, replica_groups=mesh['groups'=2,'range'=8,'chan'=2] {'range'}, dimensions={1} | all-to-all | bytes 4194304 | tf_op jit(solution)/shard_map/all_to_all | solution.py:106
  105.4 1.2 %slice_bitcast_fusion = (bf16[2048,256]{1,0:T(8,128)(2,1)}, bf16[2,256,8,128]{3,2,0,1:T(8,128)(2,1)S(1)}) fusion(bf16[2048,1,512]{2,0,1:T(8,128)(2,1)S(1)} %bitcast.71), kind=kLoop, calls=%fused_computation.12 | loop fusion | bytes 4194304 | tf_op jit(solution)/shard_map/squeeze | solution.py:108
  106.6 0.0 collective-permute-start
  106.7 1.0 copy.46
  107.7 1.9 %collective-permute-done = bf16[2048,256]{1,0:T(8,128)(2,1)} collective-permute-done((bf16[2048,256]{1,0:T(8,128)(2,1)}, bf16[2048,256]{1,0:T(8,128)(2,1)}, u32[]{:S(2)}, u32[]{:S(2)}) %collective-permute-start) | collective-permute-done | bytes 1048608 | tf_op jit(solution)/shard_map/ppermute | solution.py:112
  109.6 1.4 %broadcast_select_fusion.1 = (bf16[2048,256]{1,0:T(8,128)(2,1)S(1)}, bf16[2048,256]{1,0:T(8,128)(2,1)S(1)}) fusion(bf16[2048,256]{1,0:T(8,128)(2,1)} %collective-permute-done, pred[]{:T(512)S(6)} %eq.19, bf16[2048,1,512]{2,0,1:T(8,128)(2,1)S(1)} %bitcast.72), kind=kLoop, calls=%fused_computation.15 | loop fusion | flops 1048576 | bytes 4194305 | tf_op jit(solution)/shard_map/jit(_where)/select_n | solution.py:115
  111.0 4.7 %convolution_multiply_fusion = f32[512,4096]{1,0:T(8,128)} fusion(bf16[2048,256]{1,0:T(8,128)(2,1)S(1)} %get-tuple-element.13, bf16[2048,256]{1,0:T(8,128)(2,1)S(1)} %get-tuple-element.12, bf16[256,128]{0,1:T(8,128)(2,1)S(1)} %get-tuple-element.19, bf16[256,128]{0,1:T(8,128)(2,1)S(1)} %get-tuple-element.18, bf16[256,256]{0,1:T(8,128)(2,1)S(1)} %bitcast.83), kind=kOutput, calls=%fused_computation.1 | convolution fusion | flops 1080819712 | bytes 10747904 | tf_op jit(solution)/shard_map/dot_general | solution.py:121
  (8 shorter events, 0.1 us)
Async XLA Ops:
  0.6 11.1 %copy-start.1 = (f32[2,2049]{1,0:T(2,128)S(1)}, f32[2,2049]{1,0:T(2,128)}, u32[]{:S(2)}) copy-start(f32[2,2049]{1,0:T(2,128)} %param.4) | copy-start | bytes 49180
  4.5 33.0 %all-to-all-start = ((bf16[2048,1,2,128]{3,2,1,0:T(2,128)(2,1)}), bf16[2048,1,2,128]{3,2,1,0:T(2,128)(2,1)S(1)}, u32[]{:S(2)}, u32[]{:S(2)}) async-start(bf16[2048,1,2,128]{3,2,1,0:T(2,128)(2,1)} %bitcast.1), calls=%async_computation | async-start | bytes 2097152 | tf_op jit(solution)/shard_map/all_to_all | solution.py:93
  17.6 2.9 %copy-start.2 = (s32[2,8]{1,0:T(2,128)S(1)}, s32[2,8]{1,0:T(2,128)}, u32[]{:S(2)}) copy-start(s32[2,8]{1,0:T(2,128)} %param.5) | copy-start | bytes 196
  52.3 1.2 %copy-start = (bf16[32,8,8,256]{3,2,0,1:T(8,128)(2,1)S(1)}, bf16[32,8,8,256]{3,2,0,1:T(8,128)(2,1)}, u32[]{:S(2)}) copy-start(bf16[32,8,8,256]{3,2,0,1:T(8,128)(2,1)} %copy.54) | copy-start | bytes 3145732
  106.6 3.0 %collective-permute-start = (bf16[2048,256]{1,0:T(8,128)(2,1)}, bf16[2048,256]{1,0:T(8,128)(2,1)}, u32[]{:S(2)}, u32[]{:S(2)}) collective-permute-start(bf16[2048,256]{1,0:T(8,128)(2,1)} %get-tuple-element.14), channel_id=1, source_target_pairs={{0,1},{1,0},{2,3},{3,2},{4,5},{5,4},{6,7},{7,6},{8,9},{9,8},{10,11... | collective-permute-start | bytes 3145736 | tf_op jit(solution)/shard_map/ppermute | solution.py:112

commit v4 on v3

v4 whole, which is shorter than its diff:
```python
from functools import partial

import jax
import jax.numpy as jnp
from jax import lax
from jax.experimental import pallas as pl
from jax.experimental.pallas import tpu as pltpu
from jax.sharding import PartitionSpec as P

TRAIN = 128
BLOCK = 128


def train_cells(gates, count):
    starts = gates[0]
    widths = gates[1]
    ends = jnp.cumsum(widths)
    places = jnp.arange(count, dtype=jnp.int32)
    which = jnp.sum((ends[None, :] <= places[:, None]).astype(jnp.int32), axis=1)
    onehot = jnp.arange(gates.shape[1], dtype=jnp.int32)[None, :] == which[:, None]
    offset = jnp.sum(jnp.where(onehot, (starts - (ends - widths))[None, :], 0), axis=1)
    return offset + places


def toeplitz_blocks(chirp, lags):
    taps = chirp.shape[1]
    length = BLOCK * lags + BLOCK - 1
    pad_after = max(0, length - (BLOCK - 1) - taps)
    u = jnp.pad(chirp, ((0, 0), (BLOCK - 1, pad_after)))[:, :length]
    tiled = jnp.tile(u, (1, BLOCK + 1))[:, : BLOCK * (length + 1)]
    windows = tiled.reshape(2, BLOCK, length + 1)[:, :, : BLOCK * lags]
    full = windows[:, ::-1, :]
    blocks = full.reshape(2, BLOCK, lags, BLOCK).transpose(0, 2, 1, 3)
    t_re = blocks[0]
    t_im = blocks[1]
    top = jnp.concatenate([t_re, t_im], axis=2)
    bottom = jnp.concatenate([-t_im, t_re], axis=2)
    w = jnp.concatenate([top, bottom], axis=1)
    hi = w.astype(jnp.bfloat16)
    lo = (w - hi.astype(jnp.float32)).astype(jnp.bfloat16)
    return jnp.concatenate([hi, lo], axis=2)


def conv_kernel(x_ref, w_ref, o_ref, *, lags):
    d = pl.program_id(0)
    start = pl.multiple_of(d * BLOCK, BLOCK)
    span = lags * BLOCK
    acc = jnp.dot(x_ref[0, :, pl.ds(start, span)], w_ref[0], preferred_element_type=jnp.float32)
    acc = acc + jnp.dot(
        x_ref[1, :, pl.ds(start, span)], w_ref[1], preferred_element_type=jnp.float32
    )
    out = acc[:, : 2 * BLOCK] + acc[:, 2 * BLOCK :]
    o_ref[0] = out[:, :BLOCK].astype(o_ref.dtype)
    o_ref[1] = out[:, BLOCK:].astype(o_ref.dtype)


def causal_filter(x, w):
    _, rows, total = x.shape
    lags = w.shape[0]
    nblocks = total // BLOCK
    flipped = w[::-1]
    stacked = jnp.stack(
        [
            flipped[:, :BLOCK].reshape(lags * BLOCK, 4 * BLOCK),
            flipped[:, BLOCK:].reshape(lags * BLOCK, 4 * BLOCK),
        ]
    )
    padded = jnp.pad(x, ((0, 0), (0, 0), ((lags - 1) * BLOCK, 0)))
    work = 2 * rows * lags * BLOCK * 4 * BLOCK * 2 * nblocks
    return pl.pallas_call(
        partial(conv_kernel, lags=lags),
        out_shape=jax.ShapeDtypeStruct((2, rows, total), jnp.bfloat16),
        grid=(nblocks,),
        in_specs=[
            pl.BlockSpec(padded.shape, lambda d: (0, 0, 0)),
            pl.BlockSpec(stacked.shape, lambda d: (0, 0, 0)),
        ],
        out_specs=pl.BlockSpec((2, rows, BLOCK), lambda d: (0, 0, d)),
        compiler_params=pltpu.CompilerParams(vmem_limit_bytes=48 * 1024 * 1024),
        cost_estimate=pl.CostEstimate(
            flops=work, transcendentals=0, bytes_accessed=2 * x.size * 2 + w.size * 2
        ),
    )(padded, stacked)


def on_device(echoes, chirp, gates):
    chans = echoes.shape[1]
    pulses = echoes.shape[2]
    cells_dev = echoes.shape[3]
    taps = chirp.shape[1]
    ranks = lax.axis_size("range")
    range_len = cells_dev * ranks
    nblocks = range_len // BLOCK
    lags = min((taps - 1 + BLOCK - 1) // BLOCK + 1, nblocks)
    series_total = chans * pulses
    series_dev = series_total // ranks

    w = toeplitz_blocks(chirp, lags)

    local = echoes.reshape(2, series_total, cells_dev)
    x = lax.all_to_all(local, "range", split_axis=1, concat_axis=2, tiled=True)
    y = causal_filter(x, w)

    cells = train_cells(gates, TRAIN)
    pick = (jnp.arange(range_len, dtype=jnp.int32)[:, None] == cells[None, :]).astype(y.dtype)
    snap = jnp.dot(
        y.reshape(2 * series_dev, range_len), pick, preferred_element_type=jnp.float32
    ).astype(y.dtype).reshape(2, series_dev, TRAIN)

    spread = jnp.broadcast_to(snap[:, :, None, :], (2, series_dev, ranks, TRAIN))
    both = jnp.concatenate([y.reshape(2, series_dev, ranks, cells_dev), spread], axis=3)
    arrived = lax.all_to_all(both, "range", split_axis=2, concat_axis=1, tiled=True)
    compressed = arrived[:, :, 0, :cells_dev].reshape(2, chans, pulses, cells_dev)
    half = arrived[:, :, 0, cells_dev:]

    partner = lax.ppermute(half, "chan", [(0, 1), (1, 0)])
    upper = lax.axis_index("chan") == 0
    every = jnp.concatenate(
        [jnp.where(upper, half, partner), jnp.where(upper, partner, half)], axis=1
    )

    left = jnp.stack([snap, jnp.stack([snap[1], -snap[0]])])
    gram = lax.dot_general(
        left, every, (((1, 3), (0, 2)), ((), ())), preferred_element_type=jnp.float32
    )
    covariance = (gram * (1.0 / TRAIN)).reshape(2, 1, series_dev, -1)
    return (compressed, covariance)


def solution(mesh):
    placed = (P("groups", "chan", None, "range"), P(), P("groups", None))
    return jax.shard_map(
        on_device,
        mesh=mesh,
        in_specs=placed,
        out_specs=(P("groups", "chan", None, "range"), P("groups", "chan", "range", None)),
        check_vma=False,
    )
```

time: 116 us -> 107 us (0.922)
  local copies, waits for them, and re-layouts: 24.2 us -> 14.5 us
  waiting for transfers between devices: 18.5 us -> 16.7 us
  other arithmetic: 2.61 us -> 4.4 us
    reshape x6 -> x2, local copies, waits for them, and re-layouts: 5.75 us -> 0.27 us  [the longest x1 0.26 us: on_device(): y.reshape(2, series_dev, ranks, cells_dev)]
    rev x2 -> x0, local copies, waits for them, and re-layouts: 4.33 us -> none  [causal_filter(): stacked = w[::-1].reshape(lags * width, 2 * width)]
    slice x0 -> x4, local copies, waits for them, and re-layouts: none -> 3.98 us  [the longest x2 2.6 us: causal_filter(): flipped[:, :BLOCK].reshape(lags * BLOCK, 4 * BLOCK)]
    all_to_all x1, waiting for transfers between devices: 16.6 us -> 13.9 us  [on_device(): x = lax.all_to_all(local, 'range', split_axis=1, concat_axis=2, tiled=True)]
    unnamed x10 -> x7, local copies, waits for them, and re-layouts: 6.05 us -> 4.23 us
    another operation x1 -> x3, other arithmetic: 0.18 us -> 1.93 us  [the longest x1 1.73 us: causal_filter(): jnp.stack([flipped[:, :BLOCK].reshape(lags * BLOCK, 4 * BLOCK), flipped[:...]
    all_to_all x2 -> x3, local copies, waits for them, and re-layouts: 2.19 us -> 0.56 us  [the longest x2 0.42 us: on_device(): x = lax.all_to_all(local, 'range', split_axis=1, concat_axis=2, tiled=True)]
    concatenate x1, other arithmetic: 0.14 us -> 1.51 us  [toeplitz_blocks(): return jnp.concatenate([hi, lo], axis=2)]
  transfers between devices with their start and end apart: 2 -> 2, of which waited for: 2 -> 2; matrix products, arithmetic and copies ran while one was open for 9% -> 11% of each run, Pallas kernels for 0% -> 0%
where the time goes in v4:
time: 107 us
  blocking collectives  51.8 us (48%)
  waiting for transfers between devices  16.7 us (16%)
  local copies, waits for them, and re-layouts  14.5 us (14%)
  starting transfers between devices  7.26 us (7%)
  Pallas kernels  6.02 us (6%)
  matrix products  5.15 us (5%)
  other arithmetic  4.4 us (4%)
    all_to_all x1, blocking collectives, on_device(): lax.all_to_all(both, 'range', split_axis=2, concat_axis=1, tiled=True)  51.8 us
    all_to_all x1, waiting for transfers between devices, on_device(): x = lax.all_to_all(local, 'range', split_axis=1, concat_axis=2, tiled=True)  13.9 us
    all_to_all x1, starting transfers between devices, on_device(): x = lax.all_to_all(local, 'range', split_axis=1, concat_axis=2, tiled=True)  7.25 us
    pallas_call x1, Pallas kernels, causal_filter(): pl.pallas_call(partial(conv_kernel, lags=lags), out_shape=jax.ShapeDtypeS...  6.02 us
    dot_general x1, matrix products, on_device(): lax.dot_general(left, every, (((1, 3), (0, 2)), ((), ())), preferred_elem...  4.69 us
    unnamed x7, local copies, waits for them, and re-layouts  4.23 us
    ppermute x1, waiting for transfers between devices, on_device(): partner = lax.ppermute(half, 'chan', [(0, 1), (1, 0)])  2.83 us
    slice x2, local copies, waits for them, and re-layouts, causal_filter(): flipped[:, :BLOCK].reshape(lags * BLOCK, 4 * BLOCK)  2.6 us
  transfers between devices with their start and end apart: 2, of which 2 were waited for; matrix products, arithmetic and copies ran while one was open for 11% of the time, Pallas kernels for 0%

profile of v4, /device:TPU:0, one launch (start us, length us, event | category | flops | bytes accessed | tf_op | source)
XLA Modules:
  0.0 106.6 jit_solution(17833729679370676521)
XLA Ops:
  0.6 0.0 copy-start
  0.6 3.8 %copy.22 = bf16[2,256,8,128]{3,0,2,1:T(2,128)(2,1)} copy(bf16[2,256,8,128]{3,2,1,0:T(8,128)(2,1)} %param.3) | data formatting | bytes 2097152 | tf_op args[0]
  4.5 7.3 %all-to-all-start = ((bf16[2,2048,128]{2,0,1:T(2,128)(2,1)}), bf16[2,2048,128]{2,0,1:T(2,128)(2,1)S(1)}, u32[]{:S(2)}, u32[]{:S(2)}) async-start(bf16[2,2048,128]{2,0,1:T(2,128)(2,1)} %bitcast), calls=%async_computation | async-start | bytes 2097152 | tf_op jit(solution)/shard_map/all_to_all | solution.py:101
  11.7 0.0 copy-done
  11.7 0.1 pad_slice_fusion.2
  11.8 0.1 tile.4
  11.9 1.6 %tile.10 = f32[2,148479]{1,0:T(2,128)S(1)} reshape(f32[2,129,1151]{2,1,0:T(8,128)S(1)} %tile.4) | data formatting | bytes 2375664 | tf_op jit(solution)/shard_map/tile | solution.py:30
  13.5 0.1 slice.65
  13.6 0.1 copy.39
  13.7 0.1 slice.66
  13.8 0.3 copy.32
  14.1 1.4 %rev.4 = f32[2,128,1024]{1,2,0:T(8,128)S(1)} reverse(f32[2,128,1024]{1,2,0:T(8,128)S(1)} %copy.32), dimensions={1} | reverse | bytes 2097152 | tf_op jit(solution)/shard_map/rev | solution.py:32
  15.6 0.1 fusion.13
  15.6 0.1 slice_bitcast_fusion.2
  15.7 0.1 subtract_convert_fusion
  15.9 0.1 fusion.3
  16.0 1.5 %fusion.4 = (bf16[8,128,512]{1,2,0:T(8,128)(2,1)}, bf16[8,128,512]{1,2,0:T(8,128)(2,1)S(1)}) fusion(bf16[8,256,256]{1,2,0:T(8,128)(2,1)S(1)} %fusion.3, bf16[8,256,256]{1,2,0:T(8,128)(2,1)S(1)} %subtract_convert_fusion), kind=kLoop, calls=%fused_computation.14 | loop fusion | flops 4194304 | bytes 4194304 | tf_op jit(solution)/shard_map/concatenate | solution.py:41
  17.5 1.3 %slice.55 = bf16[8,128,512]{1,2,0:T(8,128)(2,1)S(1)} reverse(bf16[8,128,512]{1,2,0:T(8,128)(2,1)} %get-tuple-element.14), dimensions={0} | reverse | bytes 2097152 | tf_op jit(solution)/shard_map/slice | solution.py:64
  18.8 1.3 %copy.26 = bf16[8,128,512]{2,1,0:T(8,128)(2,1)} copy(bf16[8,128,512]{1,2,0:T(8,128)(2,1)S(1)} %slice.55) | data formatting | bytes 2097152 | tf_op jit(solution)/shard_map/slice | solution.py:64
  20.1 0.0 copy-start.1
  20.1 0.1 slice.57
  20.2 1.3 %copy.27 = bf16[8,128,512]{2,1,0:T(8,128)(2,1)} copy(bf16[8,128,512]{1,2,0:T(8,128)(2,1)S(1)} %slice.57) | data formatting | bytes 2097152 | tf_op jit(solution)/shard_map/slice | solution.py:65
  21.5 0.0 copy-done.1
  21.5 0.2 reduce-window.4
  21.7 0.1 convert_reduce_fusion
  21.8 0.1 select_reduce_fusion
  21.9 1.7 %pad_maximum_fusion.w_ref = bf16[2,1024,512]{2,1,0:T(8,128)(2,1)S(1)} fusion(bf16[1,1024,512]{2,1,0:T(8,128)(2,1)} %bitcast.84, bf16[1,1024,512]{2,1,0:T(8,128)(2,1)} %bitcast.83), kind=kLoop, calls=%fused_computation.5 | loop fusion | flops 1048576 | bytes 4194304 | tf_op jit(solution)/shard_map/stack | solution.py:62
  23.6 13.9 %all-to-all-done = bf16[2,2048,128]{2,0,1:T(2,128)(2,1)S(1)} async-done(((bf16[2,2048,128]{2,0,1:T(2,128)(2,1)}), bf16[2,2048,128]{2,0,1:T(2,128)(2,1)S(1)}, u32[]{:S(2)}, u32[]{:S(2)}) %all-to-all-start) | async-done | bytes 1048608 | tf_op jit(solution)/shard_map/all_to_all | solution.py:101
  37.5 0.1 copy.23
  37.6 0.3 copy.40
  37.9 0.1 pad.8.x_ref
  38.1 6.0 %shard_map.50 = bf16[2,256,1024]{2,1,0:T(8,128)(2,1)S(1)} custom-call(bf16[2,256,1920]{2,1,0:T(8,128)(2,1)S(1)} %pad.8.x_ref, bf16[2,1024,512]{2,1,0:T(8,128)(2,1)S(1)} %pad_maximum_fusion.w_ref), custom_call_target="tpu_custom_call" | custom-call | flops 4294967296 | bytes 4194304 | tf_op jit(solution)/shard_map/pallas_call | solution.py:70
  44.1 0.3 copy_bitcast_fusion.2
  44.4 0.5 convolution_convert_fusion
  44.8 0.2 broadcast_in_dim.32
  45.0 0.3 pad_maximum_fusion.1
  45.3 51.8 %all_to_all.36 = bf16[2,256,8,256]{3,1,0,2:T(8,128)(2,1)S(1)} all-to-all(bf16[2,256,8,256]{3,1,0,2:T(8,128)(2,1)S(1)} %pad_maximum_fusion.1), channel_id=1, replica_groups=mesh['groups'=2,'range'=8,'chan'=2] {'range'}, dimensions={2} | all-to-all | bytes 4194304 | tf_op jit(solution)/shard_map/all_to_all | solution.py:112
  97.1 0.1 copy.29
  97.2 1.7 %slice_bitcast_fusion = (bf16[2,2048,128]{2,1,0:T(8,128)(2,1)}, bf16[2,256,8,128]{3,2,1,0:T(8,128)(2,1)}) fusion(bf16[2,2048,1,256]{3,1,0,2:T(8,128)(2,1)S(1)} %bitcast.74), kind=kLoop, calls=%fused_computation.17 | loop fusion | bytes 4194304 | tf_op jit(solution)/shard_map/squeeze | solution.py:114
  98.9 0.0 collective-permute-start
  99.0 2.8 %collective-permute-done = bf16[2,2048,128]{2,1,0:T(8,128)(2,1)S(1)} collective-permute-done((bf16[2,2048,128]{2,1,0:T(8,128)(2,1)}, bf16[2,2048,128]{2,1,0:T(8,128)(2,1)S(1)}, u32[]{:S(2)}, u32[]{:S(2)}) %collective-permute-start) | collective-permute-done | bytes 1048608 | tf_op jit(solution)/shard_map/ppermute | solution.py:116
  101.8 0.1 broadcast_select_fusion.1
  101.9 4.7 %fusion = f32[2,1,256,4096]{3,2,1,0:T(8,128)} fusion(bf16[2,2048,128]{2,1,0:T(8,128)(2,1)S(1)} %get-tuple-element.11, bf16[2,2048,128]{2,1,0:T(8,128)(2,1)S(1)} %get-tuple-element.10, bf16[1,2,256,128]{3,2,1,0:T(8,128)(2,1)S(1)} %maximum_bitcast_fusion.2, bf16[1,2,256,128]{3,2,1,0:T(8,128)(2,1)S(1)} %bitcast.86), kind=kOutput, calls=%fused_computation.1 | convolution fusion | flops 1080164352 | bytes 10747904 | tf_op jit(solution)/shard_map/dot_general | solution.py:123
  (5 shorter events, 0.0 us)
Async XLA Ops:
  0.6 11.1 %copy-start = (f32[2,2049]{1,0:T(2,128)S(1)}, f32[2,2049]{1,0:T(2,128)}, u32[]{:S(2)}) copy-start(f32[2,2049]{1,0:T(2,128)} %param.4) | copy-start | bytes 49180
  4.5 33.0 %all-to-all-start = ((bf16[2,2048,128]{2,0,1:T(2,128)(2,1)}), bf16[2,2048,128]{2,0,1:T(2,128)(2,1)S(1)}, u32[]{:S(2)}, u32[]{:S(2)}) async-start(bf16[2,2048,128]{2,0,1:T(2,128)(2,1)} %bitcast), calls=%async_computation | async-start | bytes 2097152 | tf_op jit(solution)/shard_map/all_to_all | solution.py:101
  20.1 1.4 %copy-start.1 = (s32[2,8]{1,0:T(2,128)S(1)}, s32[2,8]{1,0:T(2,128)}, u32[]{:S(2)}) copy-start(s32[2,8]{1,0:T(2,128)} %param.5) | copy-start | bytes 196
  98.9 2.9 %collective-permute-start = (bf16[2,2048,128]{2,1,0:T(8,128)(2,1)}, bf16[2,2048,128]{2,1,0:T(8,128)(2,1)S(1)}, u32[]{:S(2)}, u32[]{:S(2)}) collective-permute-start(bf16[2,2048,128]{2,1,0:T(8,128)(2,1)} %get-tuple-element.12), channel_id=1, source_target_pairs={{0,1},{1,0},{2,3},{3,2},{4,5},{5,4},{6,7},{7,6},{8,9},{9,8},{10,11... | collective-permute-start | bytes 3145736 | tf_op jit(solution)/shard_map/ppermute | solution.py:116

commit v5 on v4

--- a/solution.py
+++ b/solution.py
@@ -108,10 +108,11 @@
     ).astype(y.dtype).reshape(2, series_dev, TRAIN)
 
     spread = jnp.broadcast_to(snap[:, :, None, :], (2, series_dev, ranks, TRAIN))
-    both = jnp.concatenate([y.reshape(2, series_dev, ranks, cells_dev), spread], axis=3)
-    arrived = lax.all_to_all(both, "range", split_axis=2, concat_axis=1, tiled=True)
-    compressed = arrived[:, :, 0, :cells_dev].reshape(2, chans, pulses, cells_dev)
-    half = arrived[:, :, 0, cells_dev:]
+    half = lax.all_to_all(spread, "range", split_axis=2, concat_axis=1, tiled=True)[:, :, 0]
+    home = lax.all_to_all(
+        y.reshape(2, series_dev, ranks, cells_dev), "range", split_axis=2, concat_axis=1, tiled=True
+    )
+    compressed = home.reshape(2, chans, pulses, cells_dev)
 
     partner = lax.ppermute(half, "chan", [(0, 1), (1, 0)])
     upper = lax.axis_index("chan") == 0

time: 107 us -> 111 us (1.037)
  blocking collectives: 51.8 us -> 0 us
  waiting for transfers between devices: 16.7 us -> 64.3 us
  starting transfers between devices: 7.26 us -> 14.6 us
  local copies, waits for them, and re-layouts: 14.5 us -> 15.8 us
    all_to_all x1 -> x0, blocking collectives: 51.8 us -> none  [on_device(): lax.all_to_all(both, 'range', split_axis=2, concat_axis=1, tiled=True)]
    all_to_all x0 -> x2, waiting for transfers between devices: none -> 50.4 us  [the longest x1 25.7 us: on_device(): lax.all_to_all(y.reshape(2, series_dev, ranks, cells_dev), 'range', split...]
    all_to_all x0 -> x2, starting transfers between devices: none -> 7.23 us  [the longest x1 3.64 us: on_device(): lax.all_to_all(y.reshape(2, series_dev, ranks, cells_dev), 'range', split...]
    ppermute x1, waiting for transfers between devices: 2.83 us -> 0.01 us  [on_device(): partner = lax.ppermute(half, 'chan', [(0, 1), (1, 0)])]
    squeeze x1 -> x0, local copies, waits for them, and re-layouts: 1.68 us -> none  [on_device(): half = arrived[:, :, 0, cells_dev:]]
  transfers between devices with their start and end apart: 2 -> 4, of which waited for: 2 -> 3; matrix products, arithmetic and copies ran while one was open for 11% -> 13% of each run, Pallas kernels for 0% -> 0%
where the time goes in v5:
time: 111 us
  waiting for transfers between devices  64.3 us (58%)
  local copies, waits for them, and re-layouts  15.8 us (14%)
  starting transfers between devices  14.6 us (13%)
  Pallas kernels  6.02 us (5%)
  matrix products  5.15 us (5%)
  other arithmetic  4.11 us (4%)
    all_to_all x1, waiting for transfers between devices, on_device(): lax.all_to_all(y.reshape(2, series_dev, ranks, cells_dev), 'range', split...  25.7 us
    all_to_all x1, waiting for transfers between devices, on_device(): lax.all_to_all(spread, 'range', split_axis=2, concat_axis=1, tiled=True)  24.7 us
    all_to_all x1, waiting for transfers between devices, on_device(): x = lax.all_to_all(local, 'range', split_axis=1, concat_axis=2, tiled=True)  13.8 us
    all_to_all x1, starting transfers between devices, on_device(): x = lax.all_to_all(local, 'range', split_axis=1, concat_axis=2, tiled=True)  7.25 us
    pallas_call x1, Pallas kernels, causal_filter(): pl.pallas_call(partial(conv_kernel, lags=lags), out_shape=jax.ShapeDtypeS...  6.02 us
    dot_general x1, matrix products, on_device(): lax.dot_general(left, every, (((1, 3), (0, 2)), ((), ())), preferred_elem...  4.69 us
    unnamed x7, local copies, waits for them, and re-layouts  4.23 us
    all_to_all x1, starting transfers between devices, on_device(): lax.all_to_all(y.reshape(2, series_dev, ranks, cells_dev), 'range', split...  3.64 us
  transfers between devices with their start and end apart: 4, of which 3 were waited for; matrix products, arithmetic and copies ran while one was open for 13% of the time, Pallas kernels for 0%

profile of v5, /device:TPU:0, one launch (start us, length us, event | category | flops | bytes accessed | tf_op | source)
XLA Modules:
  0.0 110.7 jit_solution(120504257976257768)
XLA Ops:
  0.6 0.0 copy-start
  0.6 3.8 %copy.32 = bf16[2,256,8,128]{3,0,2,1:T(2,128)(2,1)} copy(bf16[2,256,8,128]{3,2,1,0:T(8,128)(2,1)} %param.3) | data formatting | bytes 2097152 | tf_op args[0]
  4.5 7.3 %all-to-all-start = ((bf16[2,2048,128]{2,0,1:T(2,128)(2,1)}), bf16[2,2048,128]{2,0,1:T(2,128)(2,1)S(1)}, u32[]{:S(2)}, u32[]{:S(2)}) async-start(bf16[2,2048,128]{2,0,1:T(2,128)(2,1)} %bitcast), calls=%async_computation | async-start | bytes 2097152 | tf_op jit(solution)/shard_map/all_to_all | solution.py:101
  11.7 0.0 copy-done
  11.7 0.1 pad_slice_fusion.2
  11.8 0.1 tile.4
  11.9 1.6 %tile.10 = f32[2,148479]{1,0:T(2,128)S(1)} reshape(f32[2,129,1151]{2,1,0:T(8,128)S(1)} %tile.4) | data formatting | bytes 2375664 | tf_op jit(solution)/shard_map/tile | solution.py:30
  13.5 0.1 slice.57
  13.6 0.1 copy.50
  13.7 0.1 slice.58
  13.8 0.3 copy.43
  14.1 1.4 %rev.4 = f32[2,128,1024]{1,2,0:T(8,128)S(1)} reverse(f32[2,128,1024]{1,2,0:T(8,128)S(1)} %copy.43), dimensions={1} | reverse | bytes 2097152 | tf_op jit(solution)/shard_map/rev | solution.py:32
  15.6 0.1 fusion.13
  15.6 0.1 slice_bitcast_fusion
  15.7 0.1 subtract_convert_fusion
  15.9 0.1 fusion.3
  16.0 1.5 %fusion.4 = (bf16[8,128,512]{1,2,0:T(8,128)(2,1)}, bf16[8,128,512]{1,2,0:T(8,128)(2,1)S(1)}) fusion(bf16[8,256,256]{1,2,0:T(8,128)(2,1)S(1)} %fusion.3, bf16[8,256,256]{1,2,0:T(8,128)(2,1)S(1)} %subtract_convert_fusion), kind=kLoop, calls=%fused_computation.13 | loop fusion | flops 4194304 | bytes 4194304 | tf_op jit(solution)/shard_map/concatenate | solution.py:41
  17.5 1.3 %slice.49 = bf16[8,128,512]{1,2,0:T(8,128)(2,1)S(1)} reverse(bf16[8,128,512]{1,2,0:T(8,128)(2,1)} %get-tuple-element.14), dimensions={0} | reverse | bytes 2097152 | tf_op jit(solution)/shard_map/slice | solution.py:64
  18.8 1.3 %copy.36 = bf16[8,128,512]{2,1,0:T(8,128)(2,1)} copy(bf16[8,128,512]{1,2,0:T(8,128)(2,1)S(1)} %slice.49) | data formatting | bytes 2097152 | tf_op jit(solution)/shard_map/slice | solution.py:64
  20.1 0.0 copy-start.1
  20.1 0.1 slice.51
  20.2 1.3 %copy.37 = bf16[8,128,512]{2,1,0:T(8,128)(2,1)} copy(bf16[8,128,512]{1,2,0:T(8,128)(2,1)S(1)} %slice.51) | data formatting | bytes 2097152 | tf_op jit(solution)/shard_map/slice | solution.py:65
  21.5 0.0 copy-done.1
  21.5 0.2 reduce-window.4
  21.7 0.1 convert_reduce_fusion
  21.8 0.1 select_reduce_fusion
  21.9 1.7 %pad_maximum_fusion.w_ref = bf16[2,1024,512]{2,1,0:T(8,128)(2,1)S(1)} fusion(bf16[1,1024,512]{2,1,0:T(8,128)(2,1)} %bitcast.81, bf16[1,1024,512]{2,1,0:T(8,128)(2,1)} %bitcast.80), kind=kLoop, calls=%fused_computation.5 | loop fusion | flops 1048576 | bytes 4194304 | tf_op jit(solution)/shard_map/stack | solution.py:62
  23.6 13.8 %all-to-all-done = bf16[2,2048,128]{2,0,1:T(2,128)(2,1)S(1)} async-done(((bf16[2,2048,128]{2,0,1:T(2,128)(2,1)}), bf16[2,2048,128]{2,0,1:T(2,128)(2,1)S(1)}, u32[]{:S(2)}, u32[]{:S(2)}) %all-to-all-start) | async-done | bytes 1048608 | tf_op jit(solution)/shard_map/all_to_all | solution.py:101
  37.5 0.1 copy.33
  37.6 0.3 copy.51
  37.9 0.1 pad.8.x_ref
  38.1 6.0 %shard_map.50 = bf16[2,256,1024]{2,1,0:T(8,128)(2,1)S(1)} custom-call(bf16[2,256,1920]{2,1,0:T(8,128)(2,1)S(1)} %pad.8.x_ref, bf16[2,1024,512]{2,1,0:T(8,128)(2,1)S(1)} %pad_maximum_fusion.w_ref), custom_call_target="tpu_custom_call" | custom-call | flops 4294967296 | bytes 4194304 | tf_op jit(solution)/shard_map/pallas_call | solution.py:70
  44.1 0.5 convolution_convert_fusion
  44.6 1.2 %broadcast_in_dim.32 = bf16[2,256,8,128]{3,1,0,2:T(8,128)(2,1)} broadcast(bf16[2,256,128]{2,1,0:T(8,128)(2,1)S(1)} %bitcast.82), dimensions={0,1,3} | broadcast | bytes 1179648 | tf_op jit(solution)/shard_map/broadcast_in_dim | solution.py:110
  45.7 3.6 %all-to-all-start.2 = ((bf16[2,256,8,128]{3,1,0,2:T(8,128)(2,1)}), bf16[2,256,8,128]{3,1,0,2:T(8,128)(2,1)S(1)}, u32[]{:S(2)}, u32[]{:S(2)}) async-start(bf16[2,256,8,128]{3,1,0,2:T(8,128)(2,1)} %broadcast_in_dim.32), calls=%async_computation.2 | async-start | bytes 2097152 | tf_op jit(solution)/shard_map/all_to_all | solution.py:111
  49.3 1.2 %copy_bitcast_fusion.2 = bf16[2,256,8,128]{3,1,0,2:T(8,128)(2,1)} fusion(bf16[2,256,1024]{2,1,0:T(8,128)(2,1)S(1)} %shard_map.50), kind=kLoop, calls=%fused_computation.15 | loop fusion | bytes 2097152 | tf_op jit(solution)/shard_map/reshape | solution.py:113
  50.6 24.7 %all-to-all-done.2 = bf16[2,256,8,128]{3,1,0,2:T(8,128)(2,1)S(1)} async-done(((bf16[2,256,8,128]{3,1,0,2:T(8,128)(2,1)}), bf16[2,256,8,128]{3,1,0,2:T(8,128)(2,1)S(1)}, u32[]{:S(2)}, u32[]{:S(2)}) %all-to-all-start.2) | async-done | bytes 1048608 | tf_op jit(solution)/shard_map/all_to_all | solution.py:111
  75.3 3.6 %all-to-all-start.1 = ((bf16[2,256,8,128]{3,1,0,2:T(8,128)(2,1)}), bf16[2,256,8,128]{3,1,0,2:T(8,128)(2,1)S(1)}, u32[]{:S(2)}, u32[]{:S(2)}) async-start(bf16[2,256,8,128]{3,1,0,2:T(8,128)(2,1)} %copy_bitcast_fusion.2), calls=%async_computation.1 | async-start | bytes 2097152 | tf_op jit(solution)/shard_map/all_to_all | solution.py:112
  78.9 0.1 copy.40
  79.0 0.1 collective-permute-start
  79.1 25.7 %all-to-all-done.1 = bf16[2,256,8,128]{3,1,0,2:T(8,128)(2,1)S(1)} async-done(((bf16[2,256,8,128]{3,1,0,2:T(8,128)(2,1)}), bf16[2,256,8,128]{3,1,0,2:T(8,128)(2,1)S(1)}, u32[]{:S(2)}, u32[]{:S(2)}) %all-to-all-start.1) | async-done | bytes 1048608 | tf_op jit(solution)/shard_map/all_to_all | solution.py:112
  104.9 1.0 copy.39
  105.9 0.0 collective-permute-done
  105.9 0.1 broadcast_select_fusion.1
  106.0 4.7 %fusion = f32[2,1,256,4096]{3,2,1,0:T(8,128)} fusion(bf16[2,2048,128]{2,1,0:T(8,128)(2,1)S(1)} %get-tuple-element.13, bf16[2,2048,128]{2,1,0:T(8,128)(2,1)S(1)} %get-tuple-element.12, bf16[1,2,256,128]{3,2,1,0:T(8,128)(2,1)S(1)} %maximum_bitcast_fusion.2, bf16[1,2,256,128]{3,2,1,0:T(8,128)(2,1)S(1)} %bitcast.83), kind=kOutput, calls=%fused_computation.1 | convolution fusion | flops 1080164352 | bytes 10747904 | tf_op jit(solution)/shard_map/dot_general | solution.py:124
  (5 shorter events, 0.0 us)
Async XLA Ops:
  0.6 11.1 %copy-start = (f32[2,2049]{1,0:T(2,128)S(1)}, f32[2,2049]{1,0:T(2,128)}, u32[]{:S(2)}) copy-start(f32[2,2049]{1,0:T(2,128)} %param.4) | copy-start | bytes 49180
  4.5 33.0 %all-to-all-start = ((bf16[2,2048,128]{2,0,1:T(2,128)(2,1)}), bf16[2,2048,128]{2,0,1:T(2,128)(2,1)S(1)}, u32[]{:S(2)}, u32[]{:S(2)}) async-start(bf16[2,2048,128]{2,0,1:T(2,128)(2,1)} %bitcast), calls=%async_computation | async-start | bytes 2097152 | tf_op jit(solution)/shard_map/all_to_all | solution.py:101
  20.1 1.4 %copy-start.1 = (s32[2,8]{1,0:T(2,128)S(1)}, s32[2,8]{1,0:T(2,128)}, u32[]{:S(2)}) copy-start(s32[2,8]{1,0:T(2,128)} %param.5) | copy-start | bytes 196
  45.7 29.5 %all-to-all-start.2 = ((bf16[2,256,8,128]{3,1,0,2:T(8,128)(2,1)}), bf16[2,256,8,128]{3,1,0,2:T(8,128)(2,1)S(1)}, u32[]{:S(2)}, u32[]{:S(2)}) async-start(bf16[2,256,8,128]{3,1,0,2:T(8,128)(2,1)} %broadcast_in_dim.32), calls=%async_computation.2 | async-start | bytes 2097152 | tf_op jit(solution)/shard_map/all_to_all | solution.py:111
  75.3 29.6 %all-to-all-start.1 = ((bf16[2,256,8,128]{3,1,0,2:T(8,128)(2,1)}), bf16[2,256,8,128]{3,1,0,2:T(8,128)(2,1)S(1)}, u32[]{:S(2)}, u32[]{:S(2)}) async-start(bf16[2,256,8,128]{3,1,0,2:T(8,128)(2,1)} %copy_bitcast_fusion.2), calls=%async_computation.1 | async-start | bytes 2097152 | tf_op jit(solution)/shard_map/all_to_all | solution.py:112
  79.0 26.9 %collective-permute-start = (bf16[2,2048,128]{2,1,0:T(8,128)(2,1)S(1)}, bf16[2,2048,128]{2,1,0:T(8,128)(2,1)S(1)}, u32[]{:S(2)}, u32[]{:S(2)}) collective-permute-start(bf16[2,2048,128]{2,1,0:T(8,128)(2,1)S(1)} %bitcast.75), channel_id=1, source_target_pairs={{0,1},{1,0},{2,3},{3,2},{4,5},{5,4},{6,7},{7,6},{8,9},{9,8},{10,11... | collective-permute-start | bytes 3145736 | tf_op jit(solution)/shard_map/ppermute | solution.py:117

commit v6 on v4

--- a/solution.py
+++ b/solution.py
@@ -83,6 +83,54 @@
     )(padded, stacked)
 
 
+def gram_kernel(first_ref, left_ref, cols_ref, *rest):
+    out_ref = rest[-1]
+    for o in range(2):
+        acc = None
+        for k in range(2):
+            part = lax.dot_general(
+                left_ref[o, k],
+                cols_ref[k],
+                (((1,), (1,)), ((), ())),
+                preferred_element_type=jnp.float32,
+            )
+            acc = part if acc is None else acc + part
+        out_ref[o, 0] = acc * (1.0 / TRAIN)
+
+
+def gram_half(left, cols, first, total_cols, into=None):
+    rows = left.shape[2]
+    ncols = cols.shape[1]
+    tile = min(512, ncols)
+    steps = ncols // tile
+    operands = [left, cols]
+    in_specs = [
+        pl.BlockSpec(left.shape, lambda i, f: (0, 0, 0, 0)),
+        pl.BlockSpec((2, tile, TRAIN), lambda i, f: (0, i, 0)),
+    ]
+    aliases = {}
+    if into is not None:
+        operands.append(into)
+        in_specs.append(pl.BlockSpec(memory_space=pl.ANY))
+        aliases = {3: 0}
+    return pl.pallas_call(
+        gram_kernel,
+        out_shape=jax.ShapeDtypeStruct((2, 1, rows, total_cols), jnp.float32),
+        grid_spec=pltpu.PrefetchScalarGridSpec(
+            num_scalar_prefetch=1,
+            grid=(steps,),
+            in_specs=in_specs,
+            out_specs=pl.BlockSpec((2, 1, rows, tile), lambda i, f: (0, 0, 0, f[0] * steps + i)),
+        ),
+        input_output_aliases=aliases,
+        cost_estimate=pl.CostEstimate(
+            flops=2 * 2 * 2 * rows * ncols * TRAIN * 2,
+            transcendentals=0,
+            bytes_accessed=2 * rows * ncols * 4 + cols.size * 2,
+        ),
+    )(first, *operands)
+
+
 def on_device(echoes, chirp, gates):
     chans = echoes.shape[1]
     pulses = echoes.shape[2]
@@ -114,16 +162,11 @@
     half = arrived[:, :, 0, cells_dev:]
 
     partner = lax.ppermute(half, "chan", [(0, 1), (1, 0)])
-    upper = lax.axis_index("chan") == 0
-    every = jnp.concatenate(
-        [jnp.where(upper, half, partner), jnp.where(upper, partner, half)], axis=1
-    )
-
+    q = lax.axis_index("chan").astype(jnp.int32)
     left = jnp.stack([snap, jnp.stack([snap[1], -snap[0]])])
-    gram = lax.dot_general(
-        left, every, (((1, 3), (0, 2)), ((), ())), preferred_element_type=jnp.float32
-    )
-    covariance = (gram * (1.0 / TRAIN)).reshape(2, 1, series_dev, -1)
+    total_cols = 2 * half.shape[1]
+    own = gram_half(left, half, q.reshape(1), total_cols)
+    covariance = gram_half(left, partner, (1 - q).reshape(1), total_cols, into=own)
     return (compressed, covariance)
 
 

time: 107 us -> 111 us (1.037)
  Pallas kernels: 6.02 us -> 15.6 us
  matrix products: 5.15 us -> 0.46 us
  waiting for transfers between devices: 16.7 us -> 13.8 us
    pallas_call x0 -> x2, Pallas kernels: none -> 9.61 us  [gram_half(): pl.pallas_call(gram_kernel, out_shape=jax.ShapeDtypeStruct((2, 1, rows, t...]
    dot_general x1 -> x0, matrix products: 4.69 us -> none  [on_device(): lax.dot_general(left, every, (((1, 3), (0, 2)), ((), ())), preferred_elem...]
    ppermute x1, waiting for transfers between devices: 2.83 us -> 0.01 us  [on_device(): partner = lax.ppermute(half, 'chan', [(0, 1), (1, 0)])]
    unnamed x7 -> x11, local copies, waits for them, and re-layouts: 4.23 us -> 5.42 us
  transfers between devices with their start and end apart: 2 -> 2, of which waited for: 2 -> 1; matrix products, arithmetic and copies ran while one was open for 11% -> 11% of each run, Pallas kernels for 0% -> 4%
where the time goes in v6:
time: 111 us; the launch traced here: 110 us
  blocking collectives  51.8 us (47%)
  Pallas kernels  15.6 us (14%)
  local copies, waits for them, and re-layouts  15.4 us (14%)
  waiting for transfers between devices  13.8 us (12%)
  starting transfers between devices  7.26 us (7%)
  other arithmetic  5.06 us (5%)
    all_to_all x1, blocking collectives, on_device(): lax.all_to_all(both, 'range', split_axis=2, concat_axis=1, tiled=True)  51.8 us
    all_to_all x1, waiting for transfers between devices, on_device(): x = lax.all_to_all(local, 'range', split_axis=1, concat_axis=2, tiled=True)  13.8 us
    pallas_call x2, Pallas kernels, gram_half(): pl.pallas_call(gram_kernel, out_shape=jax.ShapeDtypeStruct((2, 1, rows, t...  9.61 us
    all_to_all x1, starting transfers between devices, on_device(): x = lax.all_to_all(local, 'range', split_axis=1, concat_axis=2, tiled=True)  7.25 us
    pallas_call x1, Pallas kernels, causal_filter(): pl.pallas_call(partial(conv_kernel, lags=lags), out_shape=jax.ShapeDtypeS...  6.02 us
    unnamed x11, local copies, waits for them, and re-layouts  5.42 us
    slice x2, local copies, waits for them, and re-layouts, causal_filter(): flipped[:, :BLOCK].reshape(lags * BLOCK, 4 * BLOCK)  2.61 us
  transfers between devices with their start and end apart: 2, of which 1 were waited for; matrix products, arithmetic and copies ran while one was open for 11% of the time, Pallas kernels for 4%

profile of v6, /device:TPU:0, one launch (start us, length us, event | category | flops | bytes accessed | tf_op | source)
XLA Modules:
  0.0 110.3 jit_solution(11902940946899390363)
XLA Ops:
  0.6 0.0 copy-start.2
  0.6 3.8 %copy.20 = bf16[2,256,8,128]{3,0,2,1:T(2,128)(2,1)} copy(bf16[2,256,8,128]{3,2,1,0:T(8,128)(2,1)} %param.3) | data formatting | bytes 2097152 | tf_op args[0]
  4.5 7.3 %all-to-all-start = ((bf16[2,2048,128]{2,0,1:T(2,128)(2,1)}), bf16[2,2048,128]{2,0,1:T(2,128)(2,1)S(1)}, u32[]{:S(2)}, u32[]{:S(2)}) async-start(bf16[2,2048,128]{2,0,1:T(2,128)(2,1)} %bitcast), calls=%async_computation | async-start | bytes 2097152 | tf_op jit(solution)/shard_map/all_to_all | solution.py:149
  11.7 0.0 copy-done.2
  11.7 0.1 pad_slice_fusion.2
  11.8 0.1 tile.4
  11.9 1.6 %tile.10 = f32[2,148479]{1,0:T(2,128)S(1)} reshape(f32[2,129,1151]{2,1,0:T(8,128)S(1)} %tile.4) | data formatting | bytes 2375664 | tf_op jit(solution)/shard_map/tile | solution.py:30
  13.5 0.1 slice.65
  13.6 0.1 copy.35
  13.7 0.1 slice.66
  13.8 0.3 copy.28
  14.1 1.4 %rev.4 = f32[2,128,1024]{1,2,0:T(8,128)S(1)} reverse(f32[2,128,1024]{1,2,0:T(8,128)S(1)} %copy.28), dimensions={1} | reverse | bytes 2097152 | tf_op jit(solution)/shard_map/rev | solution.py:32
  15.6 0.1 fusion.6
  15.6 0.1 slice_bitcast_fusion.2
  15.7 0.1 subtract_convert_fusion
  15.9 0.1 fusion
  16.0 1.5 %fusion.1 = (bf16[8,128,512]{1,2,0:T(8,128)(2,1)}, bf16[8,128,512]{1,2,0:T(8,128)(2,1)S(1)}) fusion(bf16[8,256,256]{1,2,0:T(8,128)(2,1)S(1)} %fusion, bf16[8,256,256]{1,2,0:T(8,128)(2,1)S(1)} %subtract_convert_fusion), kind=kLoop, calls=%fused_computation.9 | loop fusion | flops 4194304 | bytes 4194304 | tf_op jit(solution)/shard_map/concatenate | solution.py:41
  17.5 1.3 %slice.55 = bf16[8,128,512]{1,2,0:T(8,128)(2,1)S(1)} reverse(bf16[8,128,512]{1,2,0:T(8,128)(2,1)} %get-tuple-element.4), dimensions={0} | reverse | bytes 2097152 | tf_op jit(solution)/shard_map/slice | solution.py:64
  18.8 1.3 %copy.24 = bf16[8,128,512]{2,1,0:T(8,128)(2,1)} copy(bf16[8,128,512]{1,2,0:T(8,128)(2,1)S(1)} %slice.55) | data formatting | bytes 2097152 | tf_op jit(solution)/shard_map/slice | solution.py:64
  20.1 0.0 copy-start.3
  20.1 0.1 slice.57
  20.2 1.3 %copy.25 = bf16[8,128,512]{2,1,0:T(8,128)(2,1)} copy(bf16[8,128,512]{1,2,0:T(8,128)(2,1)S(1)} %slice.57) | data formatting | bytes 2097152 | tf_op jit(solution)/shard_map/slice | solution.py:65
  21.5 0.0 copy-done.3
  21.5 0.2 reduce-window.4
  21.7 0.1 convert_reduce_fusion
  21.8 0.1 select_reduce_fusion
  21.9 1.7 %pad_maximum_fusion.w_ref = bf16[2,1024,512]{2,1,0:T(8,128)(2,1)S(1)} fusion(bf16[1,1024,512]{2,1,0:T(8,128)(2,1)} %bitcast.69, bf16[1,1024,512]{2,1,0:T(8,128)(2,1)} %bitcast.68), kind=kLoop, calls=%fused_computation.3 | loop fusion | flops 1048576 | bytes 4194304 | tf_op jit(solution)/shard_map/stack | solution.py:62
  23.6 13.8 %all-to-all-done = bf16[2,2048,128]{2,0,1:T(2,128)(2,1)S(1)} async-done(((bf16[2,2048,128]{2,0,1:T(2,128)(2,1)}), bf16[2,2048,128]{2,0,1:T(2,128)(2,1)S(1)}, u32[]{:S(2)}, u32[]{:S(2)}) %all-to-all-start) | async-done | bytes 1048608 | tf_op jit(solution)/shard_map/all_to_all | solution.py:149
  37.5 0.1 copy.21
  37.6 0.3 copy.36
  37.9 0.1 pad.8.x_ref
  38.1 6.0 %shard_map.50 = bf16[2,256,1024]{2,1,0:T(8,128)(2,1)S(1)} custom-call(bf16[2,256,1920]{2,1,0:T(8,128)(2,1)S(1)} %pad.8.x_ref, bf16[2,1024,512]{2,1,0:T(8,128)(2,1)S(1)} %pad_maximum_fusion.w_ref), custom_call_target="tpu_custom_call" | custom-call | flops 4294967296 | bytes 4194304 | tf_op jit(solution)/shard_map/pallas_call | solution.py:70
  44.1 0.3 copy_bitcast_fusion.2
  44.4 0.5 convolution_convert_fusion
  44.8 0.2 broadcast_in_dim.32
  45.0 0.3 pad_maximum_fusion.1
  45.3 51.8 %all_to_all.36 = bf16[2,256,8,256]{3,1,0,2:T(8,128)(2,1)S(1)} all-to-all(bf16[2,256,8,256]{3,1,0,2:T(8,128)(2,1)S(1)} %pad_maximum_fusion.1), channel_id=1, replica_groups=mesh['groups'=2,'range'=8,'chan'=2] {'range'}, dimensions={2} | all-to-all | bytes 4194304 | tf_op jit(solution)/shard_map/all_to_all | solution.py:160
  97.1 0.2 copy.27
  97.3 1.3 %slice_bitcast_fusion = (bf16[2,2048,128]{2,1,0:T(8,128)(2,1)S(1)}, bf16[2,256,8,128]{3,2,1,0:T(8,128)(2,1)}) fusion(bf16[2,2048,1,256]{3,1,0,2:T(8,128)(2,1)S(1)} %bitcast.60), kind=kLoop, calls=%fused_computation.12 | loop fusion | bytes 4194304 | tf_op jit(solution)/shard_map/squeeze | solution.py:162
  98.6 0.0 copy-start
  98.6 0.0 collective-permute-start
  98.7 0.8 pad_maximum_fusion.3.left_ref
  99.5 0.2 copy-done
  99.7 4.8 %shard_map.51.rest_0_ = f32[2,1,256,4096]{3,2,1,0:T(8,128)} custom-call(s32[1]{0:T(128)} %bitcast.26.first_ref, bf16[2,2,256,128]{3,2,1,0:T(8,128)(2,1)} %pad_maximum_fusion.3.left_ref, bf16[2,2048,128]{2,1,0:T(8,128)(2,1)} %copy-done), custom_call_target="tpu_custom_call" | custom-call | flops 1073741824 | bytes 5242880 | tf_op jit(solution)/shard_map/pallas_call | solution.py:116
  104.5 0.0 collective-permute-done.cols_ref
  104.5 0.0 copy-start.1
  104.5 1.0 copy-done.1
  105.5 4.8 %shard_map.52 = f32[2,1,256,4096]{3,2,1,0:T(8,128)} custom-call(s32[1]{0:T(128)} %bitcast.20.first_ref, bf16[2,2,256,128]{3,2,1,0:T(8,128)(2,1)} %pad_maximum_fusion.3.left_ref, bf16[2,2048,128]{2,1,0:T(8,128)(2,1)} %copy-done.1, f32[2,1,256,4096]{3,2,1,0:T(8,128)} %shard_map.51.rest_0_), custom_call_target="tpu_custom_call", output_to_operand_aliasing={{}: (3, {})} | custom-call | flops 1073741824 | bytes 5242880 | tf_op jit(solution)/shard_map/pallas_call | solution.py:116
  (5 shorter events, 0.0 us)
Async XLA Ops:
  0.6 11.1 %copy-start.2 = (f32[2,2049]{1,0:T(2,128)S(1)}, f32[2,2049]{1,0:T(2,128)}, u32[]{:S(2)}) copy-start(f32[2,2049]{1,0:T(2,128)} %param.4) | copy-start | bytes 49180
  4.5 33.0 %all-to-all-start = ((bf16[2,2048,128]{2,0,1:T(2,128)(2,1)}), bf16[2,2048,128]{2,0,1:T(2,128)(2,1)S(1)}, u32[]{:S(2)}, u32[]{:S(2)}) async-start(bf16[2,2048,128]{2,0,1:T(2,128)(2,1)} %bitcast), calls=%async_computation | async-start | bytes 2097152 | tf_op jit(solution)/shard_map/all_to_all | solution.py:149
  20.1 1.4 %copy-start.3 = (s32[2,8]{1,0:T(2,128)S(1)}, s32[2,8]{1,0:T(2,128)}, u32[]{:S(2)}) copy-start(s32[2,8]{1,0:T(2,128)} %param.5) | copy-start | bytes 196
  98.6 1.1 copy-start
  98.6 5.9 %collective-permute-start = (bf16[2,2048,128]{2,1,0:T(8,128)(2,1)S(1)}, bf16[2,2048,128]{2,1,0:T(8,128)(2,1)S(1)}, u32[]{:S(2)}, u32[]{:S(2)}) collective-permute-start(bf16[2,2048,128]{2,1,0:T(8,128)(2,1)S(1)} %get-tuple-element.2.cols_ref), channel_id=1, source_target_pairs={{0,1},{1,0},{2,3},{3,2},{4,5},{5,4},{6,7},{7,6},{8,9},{9,8},{10,11... | collective-permute-start | bytes 3145736 | tf_op jit(solution)/shard_map/ppermute | solution.py:164
  104.5 1.0 copy-start.1

commit v7 on v4

--- a/solution.py
+++ b/solution.py
@@ -44,11 +44,19 @@
 def conv_kernel(x_ref, w_ref, o_ref, *, lags):
     d = pl.program_id(0)
     start = pl.multiple_of(d * BLOCK, BLOCK)
-    span = lags * BLOCK
-    acc = jnp.dot(x_ref[0, :, pl.ds(start, span)], w_ref[0], preferred_element_type=jnp.float32)
-    acc = acc + jnp.dot(
-        x_ref[1, :, pl.ds(start, span)], w_ref[1], preferred_element_type=jnp.float32
-    )
+    head = lags // 2
+
+    def window(lo, hi):
+        part = None
+        for k in range(2):
+            xs = x_ref[k, :, pl.ds(start + lo * BLOCK, (hi - lo) * BLOCK)]
+            term = jnp.dot(xs, w_ref[k, lo * BLOCK : hi * BLOCK], preferred_element_type=jnp.float32)
+            part = term if part is None else part + term
+        return part
+
+    acc = window(head, lags)
+    if head > 0:
+        acc = lax.cond(d >= lags - head, lambda a: a + window(0, head), lambda a: a, acc)
     out = acc[:, : 2 * BLOCK] + acc[:, 2 * BLOCK :]
     o_ref[0] = out[:, :BLOCK].astype(o_ref.dtype)
     o_ref[1] = out[:, BLOCK:].astype(o_ref.dtype)

time: 107 us -> 107 us (level)
  no operation moved by 1% of the time
where the time goes in v7:
time: 107 us
  blocking collectives  51.8 us (48%)
  waiting for transfers between devices  16.7 us (16%)
  local copies, waits for them, and re-layouts  14.5 us (14%)
  starting transfers between devices  7.26 us (7%)
  Pallas kernels  6.4 us (6%)
  matrix products  5.15 us (5%)
  other arithmetic  4.4 us (4%)
    all_to_all x1, blocking collectives, on_device(): lax.all_to_all(both, 'range', split_axis=2, concat_axis=1, tiled=True)  51.8 us
    all_to_all x1, waiting for transfers between devices, on_device(): x = lax.all_to_all(local, 'range', split_axis=1, concat_axis=2, tiled=True)  13.9 us
    all_to_all x1, starting transfers between devices, on_device(): x = lax.all_to_all(local, 'range', split_axis=1, concat_axis=2, tiled=True)  7.25 us
    pallas_call x1, Pallas kernels, causal_filter(): pl.pallas_call(partial(conv_kernel, lags=lags), out_shape=jax.ShapeDtypeS...  6.4 us
    dot_general x1, matrix products, on_device(): lax.dot_general(left, every, (((1, 3), (0, 2)), ((), ())), preferred_elem...  4.69 us
    unnamed x7, local copies, waits for them, and re-layouts  4.23 us
    ppermute x1, waiting for transfers between devices, on_device(): partner = lax.ppermute(half, 'chan', [(0, 1), (1, 0)])  2.83 us
    slice x2, local copies, waits for them, and re-layouts, causal_filter(): flipped[:, :BLOCK].reshape(lags * BLOCK, 4 * BLOCK)  2.6 us
  transfers between devices with their start and end apart: 2, of which 2 were waited for; matrix products, arithmetic and copies ran while one was open for 11% of the time, Pallas kernels for 0%

profile of v7, /device:TPU:0, one launch (start us, length us, event | category | flops | bytes accessed | tf_op | source)
XLA Modules:
  0.0 107.0 jit_solution(10191403950562918122)
XLA Ops:
  0.6 0.0 copy-start
  0.6 3.8 %copy.22 = bf16[2,256,8,128]{3,0,2,1:T(2,128)(2,1)} copy(bf16[2,256,8,128]{3,2,1,0:T(8,128)(2,1)} %param.3) | data formatting | bytes 2097152 | tf_op args[0]
  4.5 7.3 %all-to-all-start = ((bf16[2,2048,128]{2,0,1:T(2,128)(2,1)}), bf16[2,2048,128]{2,0,1:T(2,128)(2,1)S(1)}, u32[]{:S(2)}, u32[]{:S(2)}) async-start(bf16[2,2048,128]{2,0,1:T(2,128)(2,1)} %bitcast), calls=%async_computation | async-start | bytes 2097152 | tf_op jit(solution)/shard_map/all_to_all | solution.py:109
  11.7 0.0 copy-done
  11.7 0.1 pad_slice_fusion.2
  11.8 0.1 tile.4
  11.9 1.6 %tile.10 = f32[2,148479]{1,0:T(2,128)S(1)} reshape(f32[2,129,1151]{2,1,0:T(8,128)S(1)} %tile.4) | data formatting | bytes 2375664 | tf_op jit(solution)/shard_map/tile | solution.py:30
  13.5 0.1 slice.65
  13.6 0.1 copy.39
  13.7 0.1 slice.66
  13.8 0.3 copy.32
  14.1 1.4 %rev.4 = f32[2,128,1024]{1,2,0:T(8,128)S(1)} reverse(f32[2,128,1024]{1,2,0:T(8,128)S(1)} %copy.32), dimensions={1} | reverse | bytes 2097152 | tf_op jit(solution)/shard_map/rev | solution.py:32
  15.6 0.1 fusion.13
  15.6 0.1 slice_bitcast_fusion.2
  15.7 0.1 subtract_convert_fusion
  15.9 0.1 fusion.3
  16.0 1.5 %fusion.4 = (bf16[8,128,512]{1,2,0:T(8,128)(2,1)}, bf16[8,128,512]{1,2,0:T(8,128)(2,1)S(1)}) fusion(bf16[8,256,256]{1,2,0:T(8,128)(2,1)S(1)} %fusion.3, bf16[8,256,256]{1,2,0:T(8,128)(2,1)S(1)} %subtract_convert_fusion), kind=kLoop, calls=%fused_computation.14 | loop fusion | flops 4194304 | bytes 4194304 | tf_op jit(solution)/shard_map/concatenate | solution.py:41
  17.5 1.3 %slice.55 = bf16[8,128,512]{1,2,0:T(8,128)(2,1)S(1)} reverse(bf16[8,128,512]{1,2,0:T(8,128)(2,1)} %get-tuple-element.14), dimensions={0} | reverse | bytes 2097152 | tf_op jit(solution)/shard_map/slice | solution.py:72
  18.8 1.3 %copy.26 = bf16[8,128,512]{2,1,0:T(8,128)(2,1)} copy(bf16[8,128,512]{1,2,0:T(8,128)(2,1)S(1)} %slice.55) | data formatting | bytes 2097152 | tf_op jit(solution)/shard_map/slice | solution.py:72
  20.1 0.0 copy-start.1
  20.1 0.1 slice.57
  20.2 1.3 %copy.27 = bf16[8,128,512]{2,1,0:T(8,128)(2,1)} copy(bf16[8,128,512]{1,2,0:T(8,128)(2,1)S(1)} %slice.57) | data formatting | bytes 2097152 | tf_op jit(solution)/shard_map/slice | solution.py:73
  21.5 0.0 copy-done.1
  21.5 0.2 reduce-window.4
  21.7 0.1 convert_reduce_fusion
  21.8 0.1 select_reduce_fusion
  21.9 1.7 %pad_maximum_fusion.w_ref = bf16[2,1024,512]{2,1,0:T(8,128)(2,1)S(1)} fusion(bf16[1,1024,512]{2,1,0:T(8,128)(2,1)} %bitcast.84, bf16[1,1024,512]{2,1,0:T(8,128)(2,1)} %bitcast.83), kind=kLoop, calls=%fused_computation.5 | loop fusion | flops 1048576 | bytes 4194304 | tf_op jit(solution)/shard_map/stack | solution.py:70
  23.6 13.9 %all-to-all-done = bf16[2,2048,128]{2,0,1:T(2,128)(2,1)S(1)} async-done(((bf16[2,2048,128]{2,0,1:T(2,128)(2,1)}), bf16[2,2048,128]{2,0,1:T(2,128)(2,1)S(1)}, u32[]{:S(2)}, u32[]{:S(2)}) %all-to-all-start) | async-done | bytes 1048608 | tf_op jit(solution)/shard_map/all_to_all | solution.py:109
  37.5 0.1 copy.23
  37.6 0.3 copy.40
  37.9 0.1 pad.8.x_ref
  38.1 6.4 %shard_map.50 = bf16[2,256,1024]{2,1,0:T(8,128)(2,1)S(1)} custom-call(bf16[2,256,1920]{2,1,0:T(8,128)(2,1)S(1)} %pad.8.x_ref, bf16[2,1024,512]{2,1,0:T(8,128)(2,1)S(1)} %pad_maximum_fusion.w_ref), custom_call_target="tpu_custom_call" | custom-call | flops 4294967296 | bytes 4194304 | tf_op jit(solution)/shard_map/pallas_call | solution.py:78
  44.5 0.3 copy_bitcast_fusion.2
  44.7 0.5 convolution_convert_fusion
  45.2 0.2 broadcast_in_dim.32
  45.4 0.3 pad_maximum_fusion.1
  45.7 51.8 %all_to_all.36 = bf16[2,256,8,256]{3,1,0,2:T(8,128)(2,1)S(1)} all-to-all(bf16[2,256,8,256]{3,1,0,2:T(8,128)(2,1)S(1)} %pad_maximum_fusion.1), channel_id=1, replica_groups=mesh['groups'=2,'range'=8,'chan'=2] {'range'}, dimensions={2} | all-to-all | bytes 4194304 | tf_op jit(solution)/shard_map/all_to_all | solution.py:120
  97.5 0.1 copy.29
  97.6 1.7 %slice_bitcast_fusion = (bf16[2,2048,128]{2,1,0:T(8,128)(2,1)}, bf16[2,256,8,128]{3,2,1,0:T(8,128)(2,1)}) fusion(bf16[2,2048,1,256]{3,1,0,2:T(8,128)(2,1)S(1)} %bitcast.74), kind=kLoop, calls=%fused_computation.17 | loop fusion | bytes 4194304 | tf_op jit(solution)/shard_map/squeeze | solution.py:122
  99.3 0.0 collective-permute-start
  99.4 2.8 %collective-permute-done = bf16[2,2048,128]{2,1,0:T(8,128)(2,1)S(1)} collective-permute-done((bf16[2,2048,128]{2,1,0:T(8,128)(2,1)}, bf16[2,2048,128]{2,1,0:T(8,128)(2,1)S(1)}, u32[]{:S(2)}, u32[]{:S(2)}) %collective-permute-start) | collective-permute-done | bytes 1048608 | tf_op jit(solution)/shard_map/ppermute | solution.py:124
  102.2 0.1 broadcast_select_fusion.1
  102.3 4.7 %fusion = f32[2,1,256,4096]{3,2,1,0:T(8,128)} fusion(bf16[2,2048,128]{2,1,0:T(8,128)(2,1)S(1)} %get-tuple-element.11, bf16[2,2048,128]{2,1,0:T(8,128)(2,1)S(1)} %get-tuple-element.10, bf16[1,2,256,128]{3,2,1,0:T(8,128)(2,1)S(1)} %maximum_bitcast_fusion.2, bf16[1,2,256,128]{3,2,1,0:T(8,128)(2,1)S(1)} %bitcast.86), kind=kOutput, calls=%fused_computation.1 | convolution fusion | flops 1080164352 | bytes 10747904 | tf_op jit(solution)/shard_map/dot_general | solution.py:131
  (5 shorter events, 0.0 us)
Async XLA Ops:
  0.6 11.1 %copy-start = (f32[2,2049]{1,0:T(2,128)S(1)}, f32[2,2049]{1,0:T(2,128)}, u32[]{:S(2)}) copy-start(f32[2,2049]{1,0:T(2,128)} %param.4) | copy-start | bytes 49180
  4.5 33.0 %all-to-all-start = ((bf16[2,2048,128]{2,0,1:T(2,128)(2,1)}), bf16[2,2048,128]{2,0,1:T(2,128)(2,1)S(1)}, u32[]{:S(2)}, u32[]{:S(2)}) async-start(bf16[2,2048,128]{2,0,1:T(2,128)(2,1)} %bitcast), calls=%async_computation | async-start | bytes 2097152 | tf_op jit(solution)/shard_map/all_to_all | solution.py:109
  20.1 1.4 %copy-start.1 = (s32[2,8]{1,0:T(2,128)S(1)}, s32[2,8]{1,0:T(2,128)}, u32[]{:S(2)}) copy-start(s32[2,8]{1,0:T(2,128)} %param.5) | copy-start | bytes 196
  99.3 2.9 %collective-permute-start = (bf16[2,2048,128]{2,1,0:T(8,128)(2,1)}, bf16[2,2048,128]{2,1,0:T(8,128)(2,1)S(1)}, u32[]{:S(2)}, u32[]{:S(2)}) collective-permute-start(bf16[2,2048,128]{2,1,0:T(8,128)(2,1)} %get-tuple-element.12), channel_id=1, source_target_pairs={{0,1},{1,0},{2,3},{3,2},{4,5},{5,4},{6,7},{7,6},{8,9},{9,8},{10,11... | collective-permute-start | bytes 3145736 | tf_op jit(solution)/shard_map/ppermute | solution.py:124

commit v8 on v4

--- a/solution.py
+++ b/solution.py
@@ -36,9 +36,9 @@
     top = jnp.concatenate([t_re, t_im], axis=2)
     bottom = jnp.concatenate([-t_im, t_re], axis=2)
     w = jnp.concatenate([top, bottom], axis=1)
-    hi = w.astype(jnp.bfloat16)
-    lo = (w - hi.astype(jnp.float32)).astype(jnp.bfloat16)
-    return jnp.concatenate([hi, lo], axis=2)
+    hi = lax.reduce_precision(w, exponent_bits=8, mantissa_bits=7)
+    lo = (w - hi).astype(jnp.bfloat16)
+    return jnp.concatenate([hi.astype(jnp.bfloat16), lo], axis=2)
 
 
 def conv_kernel(x_ref, w_ref, o_ref, *, lags):

time: 107 us -> 107 us (level)
  no operation moved by 1% of the time
where the time goes in v8:
time: 107 us
  blocking collectives  51.8 us (48%)
  waiting for transfers between devices  16.6 us (16%)
  local copies, waits for them, and re-layouts  14.5 us (14%)
  starting transfers between devices  7.26 us (7%)
  Pallas kernels  6.02 us (6%)
  matrix products  5.15 us (5%)
  other arithmetic  4.5 us (4%)
    all_to_all x1, blocking collectives, on_device(): lax.all_to_all(both, 'range', split_axis=2, concat_axis=1, tiled=True)  51.8 us
    all_to_all x1, waiting for transfers between devices, on_device(): x = lax.all_to_all(local, 'range', split_axis=1, concat_axis=2, tiled=True)  13.8 us
    all_to_all x1, starting transfers between devices, on_device(): x = lax.all_to_all(local, 'range', split_axis=1, concat_axis=2, tiled=True)  7.25 us
    pallas_call x1, Pallas kernels, causal_filter(): pl.pallas_call(partial(conv_kernel, lags=lags), out_shape=jax.ShapeDtypeS...  6.02 us
    dot_general x1, matrix products, on_device(): lax.dot_general(left, every, (((1, 3), (0, 2)), ((), ())), preferred_elem...  4.69 us
    unnamed x7, local copies, waits for them, and re-layouts  4.23 us
    ppermute x1, waiting for transfers between devices, on_device(): partner = lax.ppermute(half, 'chan', [(0, 1), (1, 0)])  2.83 us
    slice x2, local copies, waits for them, and re-layouts, causal_filter(): flipped[:, :BLOCK].reshape(lags * BLOCK, 4 * BLOCK)  2.61 us
  transfers between devices with their start and end apart: 2, of which 2 were waited for; matrix products, arithmetic and copies ran while one was open for 11% of the time, Pallas kernels for 0%

profile of v8, /device:TPU:0, one launch (start us, length us, event | category | flops | bytes accessed | tf_op | source)
XLA Modules:
  0.0 106.6 jit_solution(12995329318003803222)
XLA Ops:
  0.6 0.0 copy-start
  0.6 3.8 %copy.22 = bf16[2,256,8,128]{3,0,2,1:T(2,128)(2,1)} copy(bf16[2,256,8,128]{3,2,1,0:T(8,128)(2,1)} %param.3) | data formatting | bytes 2097152 | tf_op args[0]
  4.5 7.3 %all-to-all-start = ((bf16[2,2048,128]{2,0,1:T(2,128)(2,1)}), bf16[2,2048,128]{2,0,1:T(2,128)(2,1)S(1)}, u32[]{:S(2)}, u32[]{:S(2)}) async-start(bf16[2,2048,128]{2,0,1:T(2,128)(2,1)} %bitcast), calls=%async_computation | async-start | bytes 2097152 | tf_op jit(solution)/shard_map/all_to_all | solution.py:101
  11.7 0.0 copy-done
  11.7 0.1 pad_slice_fusion.2
  11.8 0.1 tile.4
  11.9 1.6 %tile.10 = f32[2,148479]{1,0:T(2,128)S(1)} reshape(f32[2,129,1151]{2,1,0:T(8,128)S(1)} %tile.4) | data formatting | bytes 2375664 | tf_op jit(solution)/shard_map/tile | solution.py:30
  13.5 0.1 slice.65
  13.6 0.1 copy.39
  13.7 0.1 slice.66
  13.8 0.3 copy.32
  14.1 1.4 %rev.4 = f32[2,128,1024]{1,2,0:T(8,128)S(1)} reverse(f32[2,128,1024]{1,2,0:T(8,128)S(1)} %copy.32), dimensions={1} | reverse | bytes 2097152 | tf_op jit(solution)/shard_map/rev | solution.py:32
  15.6 0.1 fusion.13
  15.6 0.1 slice_bitcast_fusion.2
  15.7 0.4 reduce-precision_convert_fusion
  16.1 1.5 %fusion.4 = (bf16[8,128,512]{1,2,0:T(8,128)(2,1)}, bf16[8,128,512]{1,2,0:T(8,128)(2,1)S(1)}) fusion(bf16[8,256,256]{1,2,0:T(8,128)(2,1)S(1)} %get-tuple-element.16, bf16[8,256,256]{1,2,0:T(8,128)(2,1)S(1)} %get-tuple-element.17), kind=kLoop, calls=%fused_computation.15 | loop fusion | flops 4194304 | bytes 4194304 | tf_op jit(solution)/shard_map/concatenate | solution.py:41
  17.6 1.3 %slice.55 = bf16[8,128,512]{1,2,0:T(8,128)(2,1)S(1)} reverse(bf16[8,128,512]{1,2,0:T(8,128)(2,1)} %get-tuple-element.14), dimensions={0} | reverse | bytes 2097152 | tf_op jit(solution)/shard_map/slice | solution.py:64
  18.9 1.3 %copy.26 = bf16[8,128,512]{2,1,0:T(8,128)(2,1)} copy(bf16[8,128,512]{1,2,0:T(8,128)(2,1)S(1)} %slice.55) | data formatting | bytes 2097152 | tf_op jit(solution)/shard_map/slice | solution.py:64
  20.2 0.0 copy-start.1
  20.2 0.1 slice.57
  20.3 1.3 %copy.27 = bf16[8,128,512]{2,1,0:T(8,128)(2,1)} copy(bf16[8,128,512]{1,2,0:T(8,128)(2,1)S(1)} %slice.57) | data formatting | bytes 2097152 | tf_op jit(solution)/shard_map/slice | solution.py:65
  21.6 0.0 copy-done.1
  21.6 0.2 reduce-window.4
  21.8 0.1 convert_reduce_fusion
  21.9 0.1 select_reduce_fusion
  22.0 1.7 %pad_maximum_fusion.w_ref = bf16[2,1024,512]{2,1,0:T(8,128)(2,1)S(1)} fusion(bf16[1,1024,512]{2,1,0:T(8,128)(2,1)} %bitcast.84, bf16[1,1024,512]{2,1,0:T(8,128)(2,1)} %bitcast.83), kind=kLoop, calls=%fused_computation.8 | loop fusion | flops 1048576 | bytes 4194304 | tf_op jit(solution)/shard_map/stack | solution.py:62
  23.7 13.8 %all-to-all-done = bf16[2,2048,128]{2,0,1:T(2,128)(2,1)S(1)} async-done(((bf16[2,2048,128]{2,0,1:T(2,128)(2,1)}), bf16[2,2048,128]{2,0,1:T(2,128)(2,1)S(1)}, u32[]{:S(2)}, u32[]{:S(2)}) %all-to-all-start) | async-done | bytes 1048608 | tf_op jit(solution)/shard_map/all_to_all | solution.py:101
  37.5 0.1 copy.23
  37.6 0.3 copy.40
  37.9 0.1 pad.8.x_ref
  38.1 6.0 %shard_map.50 = bf16[2,256,1024]{2,1,0:T(8,128)(2,1)S(1)} custom-call(bf16[2,256,1920]{2,1,0:T(8,128)(2,1)S(1)} %pad.8.x_ref, bf16[2,1024,512]{2,1,0:T(8,128)(2,1)S(1)} %pad_maximum_fusion.w_ref), custom_call_target="tpu_custom_call" | custom-call | flops 4294967296 | bytes 4194304 | tf_op jit(solution)/shard_map/pallas_call | solution.py:70
  44.1 0.3 copy_bitcast_fusion.2
  44.4 0.5 convolution_convert_fusion
  44.8 0.2 broadcast_in_dim.32
  45.0 0.3 pad_maximum_fusion.1
  45.3 51.8 %all_to_all.36 = bf16[2,256,8,256]{3,1,0,2:T(8,128)(2,1)S(1)} all-to-all(bf16[2,256,8,256]{3,1,0,2:T(8,128)(2,1)S(1)} %pad_maximum_fusion.1), channel_id=1, replica_groups=mesh['groups'=2,'range'=8,'chan'=2] {'range'}, dimensions={2} | all-to-all | bytes 4194304 | tf_op jit(solution)/shard_map/all_to_all | solution.py:112
  97.1 0.1 copy.29
  97.2 1.7 %slice_bitcast_fusion = (bf16[2,2048,128]{2,1,0:T(8,128)(2,1)}, bf16[2,256,8,128]{3,2,1,0:T(8,128)(2,1)}) fusion(bf16[2,2048,1,256]{3,1,0,2:T(8,128)(2,1)S(1)} %bitcast.74), kind=kLoop, calls=%fused_computation.18 | loop fusion | bytes 4194304 | tf_op jit(solution)/shard_map/squeeze | solution.py:114
  98.9 0.0 collective-permute-start
  99.0 2.8 %collective-permute-done = bf16[2,2048,128]{2,1,0:T(8,128)(2,1)S(1)} collective-permute-done((bf16[2,2048,128]{2,1,0:T(8,128)(2,1)}, bf16[2,2048,128]{2,1,0:T(8,128)(2,1)S(1)}, u32[]{:S(2)}, u32[]{:S(2)}) %collective-permute-start) | collective-permute-done | bytes 1048608 | tf_op jit(solution)/shard_map/ppermute | solution.py:116
  101.8 0.1 broadcast_select_fusion.1
  101.9 4.7 %fusion = f32[2,1,256,4096]{3,2,1,0:T(8,128)} fusion(bf16[2,2048,128]{2,1,0:T(8,128)(2,1)S(1)} %get-tuple-element.11, bf16[2,2048,128]{2,1,0:T(8,128)(2,1)S(1)} %get-tuple-element.10, bf16[1,2,256,128]{3,2,1,0:T(8,128)(2,1)S(1)} %maximum_bitcast_fusion.2, bf16[1,2,256,128]{3,2,1,0:T(8,128)(2,1)S(1)} %bitcast.86), kind=kOutput, calls=%fused_computation.1 | convolution fusion | flops 1080164352 | bytes 10747904 | tf_op jit(solution)/shard_map/dot_general | solution.py:123
  (5 shorter events, 0.0 us)
Async XLA Ops:
  0.6 11.1 %copy-start = (f32[2,2049]{1,0:T(2,128)S(1)}, f32[2,2049]{1,0:T(2,128)}, u32[]{:S(2)}) copy-start(f32[2,2049]{1,0:T(2,128)} %param.4) | copy-start | bytes 49180
  4.5 33.0 %all-to-all-start = ((bf16[2,2048,128]{2,0,1:T(2,128)(2,1)}), bf16[2,2048,128]{2,0,1:T(2,128)(2,1)S(1)}, u32[]{:S(2)}, u32[]{:S(2)}) async-start(bf16[2,2048,128]{2,0,1:T(2,128)(2,1)} %bitcast), calls=%async_computation | async-start | bytes 2097152 | tf_op jit(solution)/shard_map/all_to_all | solution.py:101
  20.2 1.4 %copy-start.1 = (s32[2,8]{1,0:T(2,128)S(1)}, s32[2,8]{1,0:T(2,128)}, u32[]{:S(2)}) copy-start(s32[2,8]{1,0:T(2,128)} %param.5) | copy-start | bytes 196
  98.9 2.9 %collective-permute-start = (bf16[2,2048,128]{2,1,0:T(8,128)(2,1)}, bf16[2,2048,128]{2,1,0:T(8,128)(2,1)S(1)}, u32[]{:S(2)}, u32[]{:S(2)}) collective-permute-start(bf16[2,2048,128]{2,1,0:T(8,128)(2,1)} %get-tuple-element.12), channel_id=1, source_target_pairs={{0,1},{1,0},{2,3},{3,2},{4,5},{5,4},{6,7},{7,6},{8,9},{9,8},{10,11... | collective-permute-start | bytes 3145736 | tf_op jit(solution)/shard_map/ppermute | solution.py:116

commit v9 on v8

--- a/solution.py
+++ b/solution.py
@@ -98,7 +98,9 @@
     w = toeplitz_blocks(chirp, lags)
 
     local = echoes.reshape(2, series_total, cells_dev)
-    x = lax.all_to_all(local, "range", split_axis=1, concat_axis=2, tiled=True)
+    x = jnp.stack(
+        [lax.all_to_all(local[k], "range", split_axis=0, concat_axis=1, tiled=True) for k in range(2)]
+    )
     y = causal_filter(x, w)
 
     cells = train_cells(gates, TRAIN)

time: 107 us -> 116 us (1.084)
  starting transfers between devices: 7.26 us -> 11.4 us
  waiting for transfers between devices: 16.6 us -> 19.7 us
    all_to_all x1 -> x2, starting transfers between devices: 7.25 us -> 11.4 us  [on_device(): lax.all_to_all(local[k], 'range', split_axis=0, concat_axis=1, tiled=True)]
    unnamed x7 -> x10, local copies, waits for them, and re-layouts: 4.23 us -> 0.7 us
    all_to_all x1 -> x2, waiting for transfers between devices: 13.8 us -> 16.9 us  [on_device(): lax.all_to_all(local[k], 'range', split_axis=0, concat_axis=1, tiled=True)]
    slice x0 -> x1, local copies, waits for them, and re-layouts: none -> 2.24 us  [on_device(): local[k]]
    all_to_all x2, local copies, waits for them, and re-layouts: 0.42 us -> 1.73 us  [on_device(): lax.all_to_all(local[k], 'range', split_axis=0, concat_axis=1, tiled=True)]
    another operation x0 -> x2, local copies, waits for them, and re-layouts: none -> 1.24 us  [on_device(): jnp.stack([lax.all_to_all(local[k], 'range', split_axis=0, concat_axis=1,...]
    another operation x1 -> x2, other arithmetic: 0.18 us -> 1.36 us  [the longest x1 1.18 us: on_device(): jnp.stack([lax.all_to_all(local[k], 'range', split_axis=0, concat_axis=1,...]
  transfers between devices with their start and end apart: 2 -> 3, of which waited for: 2 -> 3; matrix products, arithmetic and copies ran while one was open for 11% -> 10% of each run, Pallas kernels for 0% -> 0%
where the time goes in v9:
time: 116 us; the launch traced here: 115 us
  blocking collectives  51.7 us (45%)
  waiting for transfers between devices  19.7 us (17%)
  local copies, waits for them, and re-layouts  14.9 us (13%)
  starting transfers between devices  11.4 us (10%)
  Pallas kernels  6.02 us (5%)
  other arithmetic  5.43 us (5%)
  matrix products  5.15 us (4%)
    all_to_all x1, blocking collectives, on_device(): lax.all_to_all(both, 'range', split_axis=2, concat_axis=1, tiled=True)  51.7 us
    all_to_all x2, waiting for transfers between devices, on_device(): lax.all_to_all(local[k], 'range', split_axis=0, concat_axis=1, tiled=True)  16.9 us
    all_to_all x2, starting transfers between devices, on_device(): lax.all_to_all(local[k], 'range', split_axis=0, concat_axis=1, tiled=True)  11.4 us
    pallas_call x1, Pallas kernels, causal_filter(): pl.pallas_call(partial(conv_kernel, lags=lags), out_shape=jax.ShapeDtypeS...  6.02 us
    dot_general x1, matrix products, on_device(): lax.dot_general(left, every, (((1, 3), (0, 2)), ((), ())), preferred_elem...  4.69 us
    ppermute x1, waiting for transfers between devices, on_device(): partner = lax.ppermute(half, 'chan', [(0, 1), (1, 0)])  2.83 us
  transfers between devices with their start and end apart: 3, of which 3 were waited for; matrix products, arithmetic and copies ran while one was open for 10% of the time, Pallas kernels for 0%

profile of v9, /device:TPU:0, one launch (start us, length us, event | category | flops | bytes accessed | tf_op | source)
XLA Modules:
  0.0 115.1 jit_solution(3480395174687515225)
XLA Ops:
  0.6 0.0 copy-start.2
  0.6 2.2 %fusion.17 = (bf16[1,256,8,128]{3,2,1,0:T(8,128)(2,1)}, bf16[1,256,8,128]{3,2,1,0:T(8,128)(2,1)}) fusion(bf16[2,256,8,128]{3,2,1,0:T(8,128)(2,1)} %param.3), kind=kLoop, calls=%fused_computation.49 | loop fusion | bytes 2097152 | tf_op jit(solution)/shard_map/slice | solution.py:102
  2.9 7.3 %all-to-all-start.1 = ((bf16[8,256,128]{2,1,0:T(8,128)(2,1)}), bf16[8,256,128]{2,1,0:T(8,128)(2,1)S(1)}, u32[]{:S(2)}, u32[]{:S(2)}) async-start(bf16[8,256,128]{2,1,0:T(8,128)(2,1)} %bitcast.2), calls=%async_computation.1 | async-start | bytes 1048576 | tf_op jit(solution)/shard_map/all_to_all | solution.py:102
  10.1 0.0 copy-done.2
  10.1 0.1 pad_slice_fusion.2
  10.2 0.1 tile.4
  10.3 1.6 %tile.10 = f32[2,148479]{1,0:T(2,128)S(1)} reshape(f32[2,129,1151]{2,1,0:T(8,128)S(1)} %tile.4) | data formatting | bytes 2375664 | tf_op jit(solution)/shard_map/tile | solution.py:30
  11.9 0.1 slice.75
  12.0 0.1 copy.38
  12.1 0.1 slice.76
  12.2 0.3 copy.33
  12.6 1.4 %rev.4 = f32[2,128,1024]{1,2,0:T(8,128)S(1)} reverse(f32[2,128,1024]{1,2,0:T(8,128)S(1)} %copy.33), dimensions={1} | reverse | bytes 2097152 | tf_op jit(solution)/shard_map/rev | solution.py:32
  14.0 0.1 fusion.16
  14.1 0.1 slice_bitcast_fusion.2
  14.1 0.0 copy-start.3
  14.1 0.4 reduce-precision_convert_fusion
  14.5 0.3 copy-done.3
  14.8 9.8 %all-to-all-done.1 = bf16[8,256,128]{2,1,0:T(8,128)(2,1)S(1)} async-done(((bf16[8,256,128]{2,1,0:T(8,128)(2,1)}), bf16[8,256,128]{2,1,0:T(8,128)(2,1)S(1)}, u32[]{:S(2)}, u32[]{:S(2)}) %all-to-all-start.1) | async-done | bytes 524320 | tf_op jit(solution)/shard_map/all_to_all | solution.py:102
  24.6 4.1 %all-to-all-start = ((bf16[8,256,128]{2,1,0:T(8,128)(2,1)}), bf16[8,256,128]{2,1,0:T(8,128)(2,1)}, u32[]{:S(2)}, u32[]{:S(2)}) async-start(bf16[8,256,128]{2,1,0:T(8,128)(2,1)} %bitcast), calls=%async_computation | async-start | bytes 1048576 | tf_op jit(solution)/shard_map/all_to_all | solution.py:102
  28.8 0.0 copy-done
  28.8 1.5 %fusion.7 = (bf16[8,128,512]{1,2,0:T(8,128)(2,1)}, bf16[8,128,512]{1,2,0:T(8,128)(2,1)S(1)}) fusion(bf16[8,256,256]{1,2,0:T(8,128)(2,1)S(1)} %get-tuple-element.16, bf16[8,256,256]{1,2,0:T(8,128)(2,1)S(1)} %get-tuple-element.17), kind=kLoop, calls=%fused_computation.19 | loop fusion | flops 4194304 | bytes 4194304 | tf_op jit(solution)/shard_map/concatenate | solution.py:41
  30.3 1.3 %slice.65 = bf16[8,128,512]{1,2,0:T(8,128)(2,1)S(1)} reverse(bf16[8,128,512]{1,2,0:T(8,128)(2,1)} %get-tuple-element.14), dimensions={0} | reverse | bytes 2097152 | tf_op jit(solution)/shard_map/slice | solution.py:64
  31.6 0.5 copy.27
  32.1 0.1 slice.67
  32.2 1.3 %copy.28 = bf16[8,128,512]{2,1,0:T(8,128)(2,1)} copy(bf16[8,128,512]{1,2,0:T(8,128)(2,1)S(1)} %slice.67) | data formatting | bytes 2097152 | tf_op jit(solution)/shard_map/slice | solution.py:65
  33.5 0.2 reduce-window.4
  33.7 0.1 convert_reduce_fusion
  33.8 0.1 select_reduce_fusion
  33.9 1.5 %pad_maximum_fusion.w_ref = bf16[2,1024,512]{2,1,0:T(8,128)(2,1)S(1)} fusion(bf16[1,1024,512]{2,1,0:T(8,128)(2,1)} %bitcast.78, bf16[1,1024,512]{2,1,0:T(8,128)(2,1)S(1)} %bitcast.77), kind=kLoop, calls=%fused_computation.11 | loop fusion | flops 1048576 | bytes 4194304 | tf_op jit(solution)/shard_map/stack | solution.py:62
  35.4 0.0 copy-done.1
  35.4 0.3 copy.25
  35.7 0.2 stack.23
  36.0 7.1 %all-to-all-done = bf16[8,256,128]{2,1,0:T(8,128)(2,1)} async-done(((bf16[8,256,128]{2,1,0:T(8,128)(2,1)}), bf16[8,256,128]{2,1,0:T(8,128)(2,1)}, u32[]{:S(2)}, u32[]{:S(2)}) %all-to-all-start) | async-done | bytes 524320 | tf_op jit(solution)/shard_map/all_to_all | solution.py:102
  43.1 1.4 %copy.24 = bf16[256,8,128]{2,1,0:T(8,128)(2,1)S(1)} copy(bf16[256,8,128]{2,0,1:T(8,128)(2,1)} %bitcast.1) | data formatting | bytes 1048576 | tf_op jit(solution)/shard_map/all_to_all | solution.py:102
  44.5 1.0 stack.22
  45.5 1.2 %fusion.6.x_ref = bf16[2,256,1920]{2,1,0:T(8,128)(2,1)S(1)} fusion(bf16[1,256,1024]{2,1,0:T(8,128)(2,1)S(1)} %stack.23, bf16[1,256,1024]{2,1,0:T(8,128)(2,1)} %stack.22), kind=kLoop, calls=%fused_computation.16 | loop fusion | flops 6881280 | bytes 3014656 | tf_op jit(solution)/shard_map/stack | solution.py:101
  46.6 6.0 %shard_map.50 = bf16[2,256,1024]{2,1,0:T(8,128)(2,1)S(1)} custom-call(bf16[2,256,1920]{2,1,0:T(8,128)(2,1)S(1)} %fusion.6.x_ref, bf16[2,1024,512]{2,1,0:T(8,128)(2,1)S(1)} %pad_maximum_fusion.w_ref), custom_call_target="tpu_custom_call" | custom-call | flops 4294967296 | bytes 4194304 | tf_op jit(solution)/shard_map/pallas_call | solution.py:70
  52.7 0.3 copy_bitcast_fusion.1
  52.9 0.5 convolution_convert_fusion
  53.4 0.2 broadcast_in_dim.32
  53.6 0.3 pad_maximum_fusion.1
  53.9 51.7 %all_to_all.50 = bf16[2,256,8,256]{3,1,0,2:T(8,128)(2,1)S(1)} all-to-all(bf16[2,256,8,256]{3,1,0,2:T(8,128)(2,1)S(1)} %pad_maximum_fusion.1), channel_id=1, replica_groups=mesh['groups'=2,'range'=8,'chan'=2] {'range'}, dimensions={2} | all-to-all | bytes 4194304 | tf_op jit(solution)/shard_map/all_to_all | solution.py:114
  105.6 0.1 copy.30
  105.8 1.7 %slice_bitcast_fusion = (bf16[2,2048,128]{2,1,0:T(8,128)(2,1)}, bf16[2,256,8,128]{3,2,1,0:T(8,128)(2,1)}) fusion(bf16[2,2048,1,256]{3,1,0,2:T(8,128)(2,1)S(1)} %bitcast.70), kind=kLoop, calls=%fused_computation.21 | loop fusion | bytes 4194304 | tf_op jit(solution)/shard_map/squeeze | solution.py:116
  107.4 0.0 collective-permute-start
  107.5 2.8 %collective-permute-done = bf16[2,2048,128]{2,1,0:T(8,128)(2,1)S(1)} collective-permute-done((bf16[2,2048,128]{2,1,0:T(8,128)(2,1)}, bf16[2,2048,128]{2,1,0:T(8,128)(2,1)S(1)}, u32[]{:S(2)}, u32[]{:S(2)}) %collective-permute-start) | collective-permute-done | bytes 1048608 | tf_op jit(solution)/shard_map/ppermute | solution.py:118
  110.3 0.1 broadcast_select_fusion.1
  110.5 4.7 %fusion = f32[2,1,256,4096]{3,2,1,0:T(8,128)} fusion(bf16[2,2048,128]{2,1,0:T(8,128)(2,1)S(1)} %get-tuple-element.11, bf16[2,2048,128]{2,1,0:T(8,128)(2,1)S(1)} %get-tuple-element.10, bf16[1,2,256,128]{3,2,1,0:T(8,128)(2,1)S(1)} %maximum_bitcast_fusion.2, bf16[1,2,256,128]{3,2,1,0:T(8,128)(2,1)S(1)} %bitcast.81), kind=kOutput, calls=%fused_computation.1 | convolution fusion | flops 1080164352 | bytes 10747904 | tf_op jit(solution)/shard_map/dot_general | solution.py:125
  (7 shorter events, 0.0 us)
Async XLA Ops:
  0.6 9.5 %copy-start.2 = (f32[2,2049]{1,0:T(2,128)S(1)}, f32[2,2049]{1,0:T(2,128)}, u32[]{:S(2)}) copy-start(f32[2,2049]{1,0:T(2,128)} %param.4) | copy-start | bytes 49180
  2.9 21.7 %all-to-all-start.1 = ((bf16[8,256,128]{2,1,0:T(8,128)(2,1)}), bf16[8,256,128]{2,1,0:T(8,128)(2,1)S(1)}, u32[]{:S(2)}, u32[]{:S(2)}) async-start(bf16[8,256,128]{2,1,0:T(8,128)(2,1)} %bitcast.2), calls=%async_computation.1 | async-start | bytes 1048576 | tf_op jit(solution)/shard_map/all_to_all | solution.py:102
  14.1 0.7 copy-start.3
  24.6 4.2 %copy-start = (bf16[8,256,128]{2,1,0:T(8,128)(2,1)}, bf16[8,256,128]{2,1,0:T(8,128)(2,1)S(1)}, u32[]{:S(2)}) copy-start(bf16[8,256,128]{2,1,0:T(8,128)(2,1)S(1)} %all-to-all-done.1) | copy-start | bytes 1572868
  24.6 18.4 %all-to-all-start = ((bf16[8,256,128]{2,1,0:T(8,128)(2,1)}), bf16[8,256,128]{2,1,0:T(8,128)(2,1)}, u32[]{:S(2)}, u32[]{:S(2)}) async-start(bf16[8,256,128]{2,1,0:T(8,128)(2,1)} %bitcast), calls=%async_computation | async-start | bytes 1048576 | tf_op jit(solution)/shard_map/all_to_all | solution.py:102
  33.9 1.5 %copy-start.1 = (bf16[8,256,128]{2,1,0:T(8,128)(2,1)S(1)}, bf16[8,256,128]{2,1,0:T(8,128)(2,1)}, u32[]{:S(2)}) copy-start(bf16[8,256,128]{2,1,0:T(8,128)(2,1)} %copy-done) | copy-start | bytes 1572868
  107.4 2.9 %collective-permute-start = (bf16[2,2048,128]{2,1,0:T(8,128)(2,1)}, bf16[2,2048,128]{2,1,0:T(8,128)(2,1)S(1)}, u32[]{:S(2)}, u32[]{:S(2)}) collective-permute-start(bf16[2,2048,128]{2,1,0:T(8,128)(2,1)} %get-tuple-element.12), channel_id=1, source_target_pairs={{0,1},{1,0},{2,3},{3,2},{4,5},{5,4},{6,7},{7,6},{8,9},{9,8},{10,11... | collective-permute-start | bytes 3145736 | tf_op jit(solution)/shard_map/ppermute | solution.py:118

commit v10 on v8

--- a/solution.py
+++ b/solution.py
@@ -42,16 +42,27 @@
 
 
 def conv_kernel(x_ref, w_ref, o_ref, *, lags):
-    d = pl.program_id(0)
-    start = pl.multiple_of(d * BLOCK, BLOCK)
+    nblocks = x_ref.shape[2] // BLOCK
     span = lags * BLOCK
-    acc = jnp.dot(x_ref[0, :, pl.ds(start, span)], w_ref[0], preferred_element_type=jnp.float32)
-    acc = acc + jnp.dot(
-        x_ref[1, :, pl.ds(start, span)], w_ref[1], preferred_element_type=jnp.float32
-    )
-    out = acc[:, : 2 * BLOCK] + acc[:, 2 * BLOCK :]
-    o_ref[0] = out[:, :BLOCK].astype(o_ref.dtype)
-    o_ref[1] = out[:, BLOCK:].astype(o_ref.dtype)
+
+    def emit(d, x_start, count):
+        acc = None
+        for k in range(2):
+            xs = x_ref[k, :, pl.ds(x_start, count * BLOCK)]
+            ws = w_ref[k, span - count * BLOCK : span]
+            term = jnp.dot(xs, ws, preferred_element_type=jnp.float32)
+            acc = term if acc is None else acc + term
+        out = acc[:, : 2 * BLOCK] + acc[:, 2 * BLOCK :]
+        cols = pl.ds(pl.multiple_of(d * BLOCK, BLOCK), BLOCK)
+        o_ref[0, :, cols] = out[:, :BLOCK].astype(o_ref.dtype)
+        o_ref[1, :, cols] = out[:, BLOCK:].astype(o_ref.dtype)
+
+    for d in range(min(lags - 1, nblocks)):
+        emit(d, 0, d + 1)
+
+    @pl.loop(lags - 1, nblocks)
+    def _(d):
+        emit(d, pl.multiple_of((d - (lags - 1)) * BLOCK, BLOCK), lags)
 
 
 def causal_filter(x, w):
@@ -65,22 +76,21 @@
             flipped[:, BLOCK:].reshape(lags * BLOCK, 4 * BLOCK),
         ]
     )
-    padded = jnp.pad(x, ((0, 0), (0, 0), ((lags - 1) * BLOCK, 0)))
-    work = 2 * rows * lags * BLOCK * 4 * BLOCK * 2 * nblocks
+    used = sum(min(d + 1, lags) for d in range(nblocks))
+    work = 2 * rows * BLOCK * 4 * BLOCK * 2 * used
     return pl.pallas_call(
         partial(conv_kernel, lags=lags),
         out_shape=jax.ShapeDtypeStruct((2, rows, total), jnp.bfloat16),
-        grid=(nblocks,),
         in_specs=[
-            pl.BlockSpec(padded.shape, lambda d: (0, 0, 0)),
-            pl.BlockSpec(stacked.shape, lambda d: (0, 0, 0)),
+            pl.BlockSpec(memory_space=pltpu.VMEM),
+            pl.BlockSpec(memory_space=pltpu.VMEM),
         ],
-        out_specs=pl.BlockSpec((2, rows, BLOCK), lambda d: (0, 0, d)),
+        out_specs=pl.BlockSpec(memory_space=pltpu.VMEM),
         compiler_params=pltpu.CompilerParams(vmem_limit_bytes=48 * 1024 * 1024),
         cost_estimate=pl.CostEstimate(
             flops=work, transcendentals=0, bytes_accessed=2 * x.size * 2 + w.size * 2
         ),
-    )(padded, stacked)
+    )(x, stacked)
 
 
 def on_device(echoes, chirp, gates):

time: 107 us -> 104 us (0.972)
  Pallas kernels: 6.02 us -> 2.85 us
    pallas_call x1, Pallas kernels: 6.02 us -> 2.85 us  [causal_filter(): pl.pallas_call(partial(conv_kernel, lags=lags), out_shape=jax.ShapeDtypeS...]
  transfers between devices with their start and end apart: 2 -> 2, of which waited for: 2 -> 2; matrix products, arithmetic and copies ran while one was open for 11% -> 12% of each run, Pallas kernels for 0% -> 0%
where the time goes in v10:
time: 104 us; the launch traced here: 103 us
  blocking collectives  51.8 us (50%)
  waiting for transfers between devices  16.6 us (16%)
  local copies, waits for them, and re-layouts  14.4 us (14%)
  starting transfers between devices  7.26 us (7%)
  matrix products  5.15 us (5%)
  other arithmetic  4.5 us (4%)
  Pallas kernels  2.85 us (3%)
    all_to_all x1, blocking collectives, on_device(): lax.all_to_all(both, 'range', split_axis=2, concat_axis=1, tiled=True)  51.8 us
    all_to_all x1, waiting for transfers between devices, on_device(): x = lax.all_to_all(local, 'range', split_axis=1, concat_axis=2, tiled=True)  13.8 us
    all_to_all x1, starting transfers between devices, on_device(): x = lax.all_to_all(local, 'range', split_axis=1, concat_axis=2, tiled=True)  7.25 us
    dot_general x1, matrix products, on_device(): lax.dot_general(left, every, (((1, 3), (0, 2)), ((), ())), preferred_elem...  4.69 us
    unnamed x7, local copies, waits for them, and re-layouts  4.23 us
    pallas_call x1, Pallas kernels, causal_filter(): pl.pallas_call(partial(conv_kernel, lags=lags), out_shape=jax.ShapeDtypeS...  2.85 us
    ppermute x1, waiting for transfers between devices, on_device(): partner = lax.ppermute(half, 'chan', [(0, 1), (1, 0)])  2.83 us
    slice x2, local copies, waits for them, and re-layouts, causal_filter(): flipped[:, :BLOCK].reshape(lags * BLOCK, 4 * BLOCK)  2.61 us
  transfers between devices with their start and end apart: 2, of which 2 were waited for; matrix products, arithmetic and copies ran while one was open for 12% of the time, Pallas kernels for 0%

profile of v10, /device:TPU:0, one launch (start us, length us, event | category | flops | bytes accessed | tf_op | source)
XLA Modules:
  0.0 103.3 jit_solution(7042010033539075343)
XLA Ops:
  0.6 0.0 copy-start
  0.6 3.8 %copy.22 = bf16[2,256,8,128]{3,0,2,1:T(2,128)(2,1)} copy(bf16[2,256,8,128]{3,2,1,0:T(8,128)(2,1)} %param.3) | data formatting | bytes 2097152 | tf_op args[0]
  4.5 7.3 %all-to-all-start = ((bf16[2,2048,128]{2,0,1:T(2,128)(2,1)}), bf16[2,2048,128]{2,0,1:T(2,128)(2,1)S(1)}, u32[]{:S(2)}, u32[]{:S(2)}) async-start(bf16[2,2048,128]{2,0,1:T(2,128)(2,1)} %bitcast), calls=%async_computation | async-start | bytes 2097152 | tf_op jit(solution)/shard_map/all_to_all | solution.py:111
  11.7 0.0 copy-done
  11.7 0.1 pad_slice_fusion.2
  11.8 0.1 tile.4
  11.9 1.6 %tile.10 = f32[2,148479]{1,0:T(2,128)S(1)} reshape(f32[2,129,1151]{2,1,0:T(8,128)S(1)} %tile.4) | data formatting | bytes 2375664 | tf_op jit(solution)/shard_map/tile | solution.py:30
  13.5 0.1 slice.65
  13.6 0.1 copy.39
  13.7 0.1 slice.66
  13.8 0.3 copy.32
  14.1 1.4 %rev.4 = f32[2,128,1024]{1,2,0:T(8,128)S(1)} reverse(f32[2,128,1024]{1,2,0:T(8,128)S(1)} %copy.32), dimensions={1} | reverse | bytes 2097152 | tf_op jit(solution)/shard_map/rev | solution.py:32
  15.6 0.1 fusion.13
  15.6 0.1 slice_bitcast_fusion.2
  15.7 0.4 reduce-precision_convert_fusion
  16.1 1.5 %fusion.4 = (bf16[8,128,512]{1,2,0:T(8,128)(2,1)}, bf16[8,128,512]{1,2,0:T(8,128)(2,1)S(1)}) fusion(bf16[8,256,256]{1,2,0:T(8,128)(2,1)S(1)} %get-tuple-element.16, bf16[8,256,256]{1,2,0:T(8,128)(2,1)S(1)} %get-tuple-element.17), kind=kLoop, calls=%fused_computation.15 | loop fusion | flops 4194304 | bytes 4194304 | tf_op jit(solution)/shard_map/concatenate | solution.py:41
  17.6 1.3 %slice.55 = bf16[8,128,512]{1,2,0:T(8,128)(2,1)S(1)} reverse(bf16[8,128,512]{1,2,0:T(8,128)(2,1)} %get-tuple-element.14), dimensions={0} | reverse | bytes 2097152 | tf_op jit(solution)/shard_map/slice | solution.py:75
  18.9 1.3 %copy.26 = bf16[8,128,512]{2,1,0:T(8,128)(2,1)} copy(bf16[8,128,512]{1,2,0:T(8,128)(2,1)S(1)} %slice.55) | data formatting | bytes 2097152 | tf_op jit(solution)/shard_map/slice | solution.py:75
  20.2 0.0 copy-start.1
  20.2 0.1 slice.57
  20.3 1.3 %copy.27 = bf16[8,128,512]{2,1,0:T(8,128)(2,1)} copy(bf16[8,128,512]{1,2,0:T(8,128)(2,1)S(1)} %slice.57) | data formatting | bytes 2097152 | tf_op jit(solution)/shard_map/slice | solution.py:76
  21.6 0.0 copy-done.1
  21.6 0.2 reduce-window.4
  21.8 0.1 convert_reduce_fusion
  21.9 0.1 select_reduce_fusion
  22.0 1.7 %pad_maximum_fusion.w_ref = bf16[2,1024,512]{2,1,0:T(8,128)(2,1)S(1)} fusion(bf16[1,1024,512]{2,1,0:T(8,128)(2,1)} %bitcast.84, bf16[1,1024,512]{2,1,0:T(8,128)(2,1)} %bitcast.83), kind=kLoop, calls=%fused_computation.8 | loop fusion | flops 1048576 | bytes 4194304 | tf_op jit(solution)/shard_map/stack | solution.py:73
  23.7 13.8 %all-to-all-done = bf16[2,2048,128]{2,0,1:T(2,128)(2,1)S(1)} async-done(((bf16[2,2048,128]{2,0,1:T(2,128)(2,1)}), bf16[2,2048,128]{2,0,1:T(2,128)(2,1)S(1)}, u32[]{:S(2)}, u32[]{:S(2)}) %all-to-all-start) | async-done | bytes 1048608 | tf_op jit(solution)/shard_map/all_to_all | solution.py:111
  37.5 0.1 copy.23
  37.6 0.3 copy.40
  37.9 2.9 %shard_map.50 = bf16[2,256,1024]{2,1,0:T(8,128)(2,1)S(1)} custom-call(bf16[2,256,1024]{2,1,0:T(8,128)(2,1)S(1)} %bitcast.74, bf16[2,1024,512]{2,1,0:T(8,128)(2,1)S(1)} %pad_maximum_fusion.w_ref), custom_call_target="tpu_custom_call" | custom-call | flops 2415919104 | bytes 4194304 | tf_op jit(solution)/shard_map/pallas_call | solution.py:81
  40.8 0.3 copy_bitcast_fusion.2
  41.0 0.5 convolution_convert_fusion
  41.5 0.2 broadcast_in_dim.32
  41.7 0.3 pad_maximum_fusion.1
  42.0 51.8 %all_to_all.36 = bf16[2,256,8,256]{3,1,0,2:T(8,128)(2,1)S(1)} all-to-all(bf16[2,256,8,256]{3,1,0,2:T(8,128)(2,1)S(1)} %pad_maximum_fusion.1), channel_id=1, replica_groups=mesh['groups'=2,'range'=8,'chan'=2] {'range'}, dimensions={2} | all-to-all | bytes 4194304 | tf_op jit(solution)/shard_map/all_to_all | solution.py:122
  93.8 0.1 copy.29
  93.9 1.7 %slice_bitcast_fusion = (bf16[2,2048,128]{2,1,0:T(8,128)(2,1)}, bf16[2,256,8,128]{3,2,1,0:T(8,128)(2,1)}) fusion(bf16[2,2048,1,256]{3,1,0,2:T(8,128)(2,1)S(1)} %bitcast.75), kind=kLoop, calls=%fused_computation.18 | loop fusion | bytes 4194304 | tf_op jit(solution)/shard_map/squeeze | solution.py:124
  95.6 0.0 collective-permute-start
  95.7 2.8 %collective-permute-done = bf16[2,2048,128]{2,1,0:T(8,128)(2,1)S(1)} collective-permute-done((bf16[2,2048,128]{2,1,0:T(8,128)(2,1)}, bf16[2,2048,128]{2,1,0:T(8,128)(2,1)S(1)}, u32[]{:S(2)}, u32[]{:S(2)}) %collective-permute-start) | collective-permute-done | bytes 1048608 | tf_op jit(solution)/shard_map/ppermute | solution.py:126
  98.5 0.1 broadcast_select_fusion.1
  98.6 4.7 %fusion = f32[2,1,256,4096]{3,2,1,0:T(8,128)} fusion(bf16[2,2048,128]{2,1,0:T(8,128)(2,1)S(1)} %get-tuple-element.11, bf16[2,2048,128]{2,1,0:T(8,128)(2,1)S(1)} %get-tuple-element.10, bf16[1,2,256,128]{3,2,1,0:T(8,128)(2,1)S(1)} %maximum_bitcast_fusion.2, bf16[1,2,256,128]{3,2,1,0:T(8,128)(2,1)S(1)} %bitcast.86), kind=kOutput, calls=%fused_computation.1 | convolution fusion | flops 1080164352 | bytes 10747904 | tf_op jit(solution)/shard_map/dot_general | solution.py:133
  (5 shorter events, 0.0 us)
Async XLA Ops:
  0.6 11.1 %copy-start = (f32[2,2049]{1,0:T(2,128)S(1)}, f32[2,2049]{1,0:T(2,128)}, u32[]{:S(2)}) copy-start(f32[2,2049]{1,0:T(2,128)} %param.4) | copy-start | bytes 49180
  4.5 33.0 %all-to-all-start = ((bf16[2,2048,128]{2,0,1:T(2,128)(2,1)}), bf16[2,2048,128]{2,0,1:T(2,128)(2,1)S(1)}, u32[]{:S(2)}, u32[]{:S(2)}) async-start(bf16[2,2048,128]{2,0,1:T(2,128)(2,1)} %bitcast), calls=%async_computation | async-start | bytes 2097152 | tf_op jit(solution)/shard_map/all_to_all | solution.py:111
  20.2 1.4 %copy-start.1 = (s32[2,8]{1,0:T(2,128)S(1)}, s32[2,8]{1,0:T(2,128)}, u32[]{:S(2)}) copy-start(s32[2,8]{1,0:T(2,128)} %param.5) | copy-start | bytes 196
  95.6 2.9 %collective-permute-start = (bf16[2,2048,128]{2,1,0:T(8,128)(2,1)}, bf16[2,2048,128]{2,1,0:T(8,128)(2,1)S(1)}, u32[]{:S(2)}, u32[]{:S(2)}) collective-permute-start(bf16[2,2048,128]{2,1,0:T(8,128)(2,1)} %get-tuple-element.12), channel_id=1, source_target_pairs={{0,1},{1,0},{2,3},{3,2},{4,5},{5,4},{6,7},{7,6},{8,9},{9,8},{10,11... | collective-permute-start | bytes 3145736 | tf_op jit(solution)/shard_map/ppermute | solution.py:126

commit v11 on v10

--- a/solution.py
+++ b/solution.py
@@ -41,8 +41,11 @@
     return jnp.concatenate([hi.astype(jnp.bfloat16), lo], axis=2)
 
 
-def conv_kernel(x_ref, w_ref, o_ref, *, lags):
+def conv_kernel(x_ref, w_ref, pick_ref, o_ref, snap_ref, *, lags):
     nblocks = x_ref.shape[2] // BLOCK
+    ranks = o_ref.shape[0]
+    own = x_ref.shape[2] // ranks
+    per_rank = own // BLOCK
     span = lags * BLOCK
 
     def emit(d, x_start, count):
@@ -53,9 +56,10 @@
             term = jnp.dot(xs, ws, preferred_element_type=jnp.float32)
             acc = term if acc is None else acc + term
         out = acc[:, : 2 * BLOCK] + acc[:, 2 * BLOCK :]
-        cols = pl.ds(pl.multiple_of(d * BLOCK, BLOCK), BLOCK)
-        o_ref[0, :, cols] = out[:, :BLOCK].astype(o_ref.dtype)
-        o_ref[1, :, cols] = out[:, BLOCK:].astype(o_ref.dtype)
+        rank = d // per_rank
+        cols = pl.ds(pl.multiple_of((d % per_rank) * BLOCK, BLOCK), BLOCK)
+        o_ref[rank, 0, :, cols] = out[:, :BLOCK].astype(o_ref.dtype)
+        o_ref[rank, 1, :, cols] = out[:, BLOCK:].astype(o_ref.dtype)
 
     for d in range(min(lags - 1, nblocks)):
         emit(d, 0, d + 1)
@@ -64,11 +68,26 @@
     def _(d):
         emit(d, pl.multiple_of((d - (lags - 1)) * BLOCK, BLOCK), lags)
 
+    for k in range(2):
+        def gather(r, acc):
+            rows = pick_ref[pl.ds(pl.multiple_of(r * own, BLOCK), own), :]
+            return acc + jnp.dot(o_ref[r, k, :, :own], rows, preferred_element_type=jnp.float32)
 
-def causal_filter(x, w):
+        picked = lax.fori_loop(
+            0, ranks, gather, jnp.zeros((x_ref.shape[1], TRAIN), jnp.float32)
+        ).astype(o_ref.dtype)
+        snap_ref[k] = picked
+
+        @pl.loop(0, ranks)
+        def _(r):
+            o_ref[r, k, :, own:] = picked
+
+
+def causal_filter(x, w, pick, ranks):
     _, rows, total = x.shape
     lags = w.shape[0]
     nblocks = total // BLOCK
+    own = total // ranks
     flipped = w[::-1]
     stacked = jnp.stack(
         [
@@ -77,20 +96,20 @@
         ]
     )
     used = sum(min(d + 1, lags) for d in range(nblocks))
-    work = 2 * rows * BLOCK * 4 * BLOCK * 2 * used
+    work = 2 * rows * BLOCK * 4 * BLOCK * 2 * used + 2 * 2 * rows * total * TRAIN
     return pl.pallas_call(
         partial(conv_kernel, lags=lags),
-        out_shape=jax.ShapeDtypeStruct((2, rows, total), jnp.bfloat16),
-        in_specs=[
-            pl.BlockSpec(memory_space=pltpu.VMEM),
-            pl.BlockSpec(memory_space=pltpu.VMEM),
-        ],
-        out_specs=pl.BlockSpec(memory_space=pltpu.VMEM),
+        out_shape=(
+            jax.ShapeDtypeStruct((ranks, 2, rows, own + TRAIN), jnp.bfloat16),
+            jax.ShapeDtypeStruct((2, rows, TRAIN), jnp.bfloat16),
+        ),
+        in_specs=[pl.BlockSpec(memory_space=pltpu.VMEM)] * 3,
+        out_specs=(pl.BlockSpec(memory_space=pltpu.VMEM), pl.BlockSpec(memory_space=pltpu.VMEM)),
         compiler_params=pltpu.CompilerParams(vmem_limit_bytes=48 * 1024 * 1024),
         cost_estimate=pl.CostEstimate(
-            flops=work, transcendentals=0, bytes_accessed=2 * x.size * 2 + w.size * 2
+            flops=work, transcendentals=0, bytes_accessed=2 * x.size * 4 + w.size * 2 + pick.size * 2
         ),
-    )(x, stacked)
+    )(x, stacked, pick)
 
 
 def on_device(echoes, chirp, gates):
@@ -109,19 +128,13 @@
 
     local = echoes.reshape(2, series_total, cells_dev)
     x = lax.all_to_all(local, "range", split_axis=1, concat_axis=2, tiled=True)
-    y = causal_filter(x, w)
+    cells = train_cells(gates, TRAIN)
+    pick = (jnp.arange(range_len, dtype=jnp.int32)[:, None] == cells[None, :]).astype(jnp.bfloat16)
+    both, snap = causal_filter(x, w, pick, ranks)
 
-    cells = train_cells(gates, TRAIN)
-    pick = (jnp.arange(range_len, dtype=jnp.int32)[:, None] == cells[None, :]).astype(y.dtype)
-    snap = jnp.dot(
-        y.reshape(2 * series_dev, range_len), pick, preferred_element_type=jnp.float32
-    ).astype(y.dtype).reshape(2, series_dev, TRAIN)
-
-    spread = jnp.broadcast_to(snap[:, :, None, :], (2, series_dev, ranks, TRAIN))
-    both = jnp.concatenate([y.reshape(2, series_dev, ranks, cells_dev), spread], axis=3)
-    arrived = lax.all_to_all(both, "range", split_axis=2, concat_axis=1, tiled=True)
-    compressed = arrived[:, :, 0, :cells_dev].reshape(2, chans, pulses, cells_dev)
-    half = arrived[:, :, 0, cells_dev:]
+    arrived = lax.all_to_all(both, "range", split_axis=0, concat_axis=0, tiled=True)
+    compressed = arrived[..., :cells_dev].transpose(1, 0, 2, 3).reshape(2, chans, pulses, cells_dev)
+    half = arrived[..., cells_dev:].transpose(1, 0, 2, 3).reshape(2, series_total, TRAIN)
 
     partner = lax.ppermute(half, "chan", [(0, 1), (1, 0)])
     upper = lax.axis_index("chan") == 0

time: 104 us -> 105 us (level)
  Pallas kernels: 2.85 us -> 5.5 us
  waiting for transfers between devices: 16.6 us -> 15.4 us
    pallas_call x1, Pallas kernels: 2.85 us -> 5.5 us  [causal_filter(): pl.pallas_call(partial(conv_kernel, lags=lags), out_shape=(jax.ShapeDtype...]
    squeeze x1 -> x0, local copies, waits for them, and re-layouts: 1.68 us -> none  [on_device(): half = arrived[:, :, 0, cells_dev:]]
    transpose x0 -> x3, local copies, waits for them, and re-layouts: none -> 1.68 us  [the longest x1 1.04 us: on_device(): arrived[..., :cells_dev].transpose(1, 0, 2, 3)]
    select_n x1, other arithmetic: 0.14 us -> 1.37 us  [on_device(): jnp.where(upper, half, partner)]
    ppermute x1, waiting for transfers between devices: 2.83 us -> 1.68 us  [on_device(): partner = lax.ppermute(half, 'chan', [(0, 1), (1, 0)])]
where the time goes in v11:
time: 105 us
  blocking collectives  51.8 us (49%)
  waiting for transfers between devices  15.4 us (15%)
  local copies, waits for them, and re-layouts  13.8 us (13%)
  starting transfers between devices  7.32 us (7%)
  other arithmetic  5.5 us (5%)
  Pallas kernels  5.5 us (5%)
  matrix products  4.69 us (4%)
    all_to_all x1, blocking collectives, on_device(): lax.all_to_all(both, 'range', split_axis=0, concat_axis=0, tiled=True)  51.8 us
    all_to_all x1, waiting for transfers between devices, on_device(): x = lax.all_to_all(local, 'range', split_axis=1, concat_axis=2, tiled=True)  13.7 us
    all_to_all x1, starting transfers between devices, on_device(): x = lax.all_to_all(local, 'range', split_axis=1, concat_axis=2, tiled=True)  7.25 us
    pallas_call x1, Pallas kernels, causal_filter(): pl.pallas_call(partial(conv_kernel, lags=lags), out_shape=(jax.ShapeDtype...  5.5 us
    dot_general x1, matrix products, on_device(): lax.dot_general(left, every, (((1, 3), (0, 2)), ((), ())), preferred_elem...  4.69 us
    unnamed x7, local copies, waits for them, and re-layouts  4.23 us
    slice x2, local copies, waits for them, and re-layouts, causal_filter(): flipped[:, :BLOCK].reshape(lags * BLOCK, 4 * BLOCK)  2.6 us
  transfers between devices with their start and end apart: 2, of which 2 were waited for; matrix products, arithmetic and copies ran while one was open for 12% of the time, Pallas kernels for 0%

profile of v11, /device:TPU:0, one launch (start us, length us, event | category | flops | bytes accessed | tf_op | source)
XLA Modules:
  0.0 104.7 jit_solution(2301017415874675748)
XLA Ops:
  0.6 0.0 copy-start
  0.6 3.8 %copy.22 = bf16[2,256,8,128]{3,0,2,1:T(2,128)(2,1)} copy(bf16[2,256,8,128]{3,2,1,0:T(8,128)(2,1)} %param.3) | data formatting | bytes 2097152 | tf_op args[0]
  4.5 7.3 %all-to-all-start = ((bf16[2,2048,128]{2,0,1:T(2,128)(2,1)}), bf16[2,2048,128]{2,0,1:T(2,128)(2,1)S(1)}, u32[]{:S(2)}, u32[]{:S(2)}) async-start(bf16[2,2048,128]{2,0,1:T(2,128)(2,1)} %bitcast), calls=%async_computation | async-start | bytes 2097152 | tf_op jit(solution)/shard_map/all_to_all | solution.py:130
  11.7 0.0 copy-done
  11.7 0.1 pad_slice_fusion.2
  11.8 0.1 tile.4
  11.9 1.6 %tile.10 = f32[2,148479]{1,0:T(2,128)S(1)} reshape(f32[2,129,1151]{2,1,0:T(8,128)S(1)} %tile.4) | data formatting | bytes 2375664 | tf_op jit(solution)/shard_map/tile | solution.py:30
  13.5 0.1 slice.60
  13.6 0.1 copy.37
  13.7 0.1 slice.61
  13.8 0.3 copy.32
  14.1 1.4 %rev.4 = f32[2,128,1024]{1,2,0:T(8,128)S(1)} reverse(f32[2,128,1024]{1,2,0:T(8,128)S(1)} %copy.32), dimensions={1} | reverse | bytes 2097152 | tf_op jit(solution)/shard_map/rev | solution.py:32
  15.6 0.1 slice_bitcast_fusion.2
  15.7 0.4 reduce-precision_convert_fusion
  16.1 1.5 %fusion.4 = (bf16[8,128,512]{1,2,0:T(8,128)(2,1)}, bf16[8,128,512]{1,2,0:T(8,128)(2,1)S(1)}) fusion(bf16[8,256,256]{1,2,0:T(8,128)(2,1)S(1)} %get-tuple-element.20, bf16[8,256,256]{1,2,0:T(8,128)(2,1)S(1)} %get-tuple-element.21), kind=kLoop, calls=%fused_computation.13 | loop fusion | flops 4194304 | bytes 4194304 | tf_op jit(solution)/shard_map/concatenate | solution.py:41
  17.6 1.3 %slice.51 = bf16[8,128,512]{1,2,0:T(8,128)(2,1)S(1)} reverse(bf16[8,128,512]{1,2,0:T(8,128)(2,1)} %get-tuple-element.18), dimensions={0} | reverse | bytes 2097152 | tf_op jit(solution)/shard_map/slice | solution.py:94
  18.9 1.3 %copy.26 = bf16[8,128,512]{2,1,0:T(8,128)(2,1)} copy(bf16[8,128,512]{1,2,0:T(8,128)(2,1)S(1)} %slice.51) | data formatting | bytes 2097152 | tf_op jit(solution)/shard_map/slice | solution.py:94
  20.2 0.0 copy-start.1
  20.2 0.1 slice.53
  20.3 1.3 %copy.27 = bf16[8,128,512]{2,1,0:T(8,128)(2,1)} copy(bf16[8,128,512]{1,2,0:T(8,128)(2,1)S(1)} %slice.53) | data formatting | bytes 2097152 | tf_op jit(solution)/shard_map/slice | solution.py:95
  21.6 0.0 copy-done.1
  21.6 0.2 reduce-window.4
  21.8 0.1 convert_reduce_fusion
  21.9 0.1 select_reduce_fusion
  22.0 1.7 %pad_maximum_fusion.w_ref = bf16[2,1024,512]{2,1,0:T(8,128)(2,1)S(1)} fusion(bf16[1,1024,512]{2,1,0:T(8,128)(2,1)} %bitcast.66, bf16[1,1024,512]{2,1,0:T(8,128)(2,1)} %bitcast.65), kind=kLoop, calls=%fused_computation.8 | loop fusion | flops 1048576 | bytes 4194304 | tf_op jit(solution)/shard_map/stack | solution.py:92
  23.7 0.1 fusion.5.pick_ref
  23.8 13.7 %all-to-all-done = bf16[2,2048,128]{2,0,1:T(2,128)(2,1)S(1)} async-done(((bf16[2,2048,128]{2,0,1:T(2,128)(2,1)}), bf16[2,2048,128]{2,0,1:T(2,128)(2,1)S(1)}, u32[]{:S(2)}, u32[]{:S(2)}) %all-to-all-start) | async-done | bytes 1048608 | tf_op jit(solution)/shard_map/all_to_all | solution.py:130
  37.5 0.1 copy.23
  37.6 0.3 copy.38
  37.9 5.5 %shard_map.50 = (bf16[8,2,256,256]{3,2,1,0:T(8,128)(2,1)S(1)}, bf16[2,256,128]{2,1,0:T(8,128)(2,1)S(1)}) custom-call(bf16[2,256,1024]{2,1,0:T(8,128)(2,1)S(1)} %bitcast.57, bf16[2,1024,512]{2,1,0:T(8,128)(2,1)S(1)} %pad_maximum_fusion.w_ref, bf16[1024,128]{1,0:T(8,128)(2,1)S(1)} %fusion.5.pick_ref), custom_call_target="tpu_custom_call" | custom-call | flops 2550136832 | bytes 6553600 | tf_op jit(solution)/shard_map/pallas_call | solution.py:100
  43.4 51.8 %all_to_all.23 = bf16[8,2,256,256]{3,2,1,0:T(8,128)(2,1)S(1)} all-to-all(bf16[8,2,256,256]{3,2,1,0:T(8,128)(2,1)S(1)} %get-tuple-element.4), channel_id=1, replica_groups=mesh['groups'=2,'range'=8,'chan'=2] {'range'}, dimensions={0} | all-to-all | bytes 4194304 | tf_op jit(solution)/shard_map/all_to_all | solution.py:135
  95.2 0.6 slice_bitcast_fusion
  95.8 0.1 copy.29
  95.8 0.1 collective-permute-start
  96.0 1.0 copy.28
  97.0 1.7 %collective-permute-done = bf16[2,2048,128]{2,1,0:T(8,128)(2,1)} collective-permute-done((bf16[2,2048,128]{2,1,0:T(8,128)(2,1)S(1)}, bf16[2,2048,128]{2,1,0:T(8,128)(2,1)}, u32[]{:S(2)}, u32[]{:S(2)}) %collective-permute-start) | collective-permute-done | bytes 1048608 | tf_op jit(solution)/shard_map/ppermute | solution.py:139
  98.7 1.4 %broadcast_select_fusion.1 = (bf16[2,2048,128]{2,1,0:T(8,128)(2,1)S(1)}, bf16[2,2048,128]{2,1,0:T(8,128)(2,1)S(1)}) fusion(bf16[2,2048,128]{2,1,0:T(8,128)(2,1)} %collective-permute-done, pred[]{:T(512)S(6)} %eq.35, bf16[2,8,256,128]{3,2,1,0:T(8,128)(2,1)S(1)} %copy.29), kind=kLoop, calls=%fused_computation.19 | loop fusion | flops 1048576 | bytes 4194305 | tf_op jit(solution)/shard_map/jit(_where)/select_n | solution.py:142
  100.1 4.7 %fusion = f32[2,1,256,4096]{3,2,1,0:T(8,128)} fusion(bf16[2,2048,128]{2,1,0:T(8,128)(2,1)S(1)} %get-tuple-element.15, bf16[2,2048,128]{2,1,0:T(8,128)(2,1)S(1)} %get-tuple-element.14, bf16[1,2,256,128]{3,2,1,0:T(8,128)(2,1)S(1)} %maximum_bitcast_fusion.2, bf16[1,2,256,128]{3,2,1,0:T(8,128)(2,1)S(1)} %bitcast.58), kind=kOutput, calls=%fused_computation.1 | convolution fusion | flops 1080164352 | bytes 10747904 | tf_op jit(solution)/shard_map/dot_general | solution.py:146
  (6 shorter events, 0.1 us)
Async XLA Ops:
  0.6 11.1 %copy-start = (f32[2,2049]{1,0:T(2,128)S(1)}, f32[2,2049]{1,0:T(2,128)}, u32[]{:S(2)}) copy-start(f32[2,2049]{1,0:T(2,128)} %param.4) | copy-start | bytes 49180
  4.5 33.0 %all-to-all-start = ((bf16[2,2048,128]{2,0,1:T(2,128)(2,1)}), bf16[2,2048,128]{2,0,1:T(2,128)(2,1)S(1)}, u32[]{:S(2)}, u32[]{:S(2)}) async-start(bf16[2,2048,128]{2,0,1:T(2,128)(2,1)} %bitcast), calls=%async_computation | async-start | bytes 2097152 | tf_op jit(solution)/shard_map/all_to_all | solution.py:130
  20.2 1.4 %copy-start.1 = (s32[2,8]{1,0:T(2,128)S(1)}, s32[2,8]{1,0:T(2,128)}, u32[]{:S(2)}) copy-start(s32[2,8]{1,0:T(2,128)} %param.5) | copy-start | bytes 196
  95.8 2.9 %collective-permute-start = (bf16[2,2048,128]{2,1,0:T(8,128)(2,1)S(1)}, bf16[2,2048,128]{2,1,0:T(8,128)(2,1)}, u32[]{:S(2)}, u32[]{:S(2)}) collective-permute-start(bf16[2,2048,128]{2,1,0:T(8,128)(2,1)S(1)} %bitcast.63), channel_id=1, source_target_pairs={{0,1},{1,0},{2,3},{3,2},{4,5},{5,4},{6,7},{7,6},{8,9},{9,8},{10,11... | collective-permute-start | bytes 3145736 | tf_op jit(solution)/shard_map/ppermute | solution.py:139
